TPU v7x, 256 devices: a whole 4x4x8 slice. The times are simulated.
256 devices in a mesh: chan: 32 (over z, x_lo, core), win: 8 (over x_hi, y).
Axes of the slice: x: 4 (x_hi: 2, x_lo: 2; x = x_hi * 2 + x_lo), y: 4, z: 8, core: 2. Of those that a mesh axis runs over, the one named last changes fastest.
Arguments:
- strain_rate: bfloat16 [8, 1024, 8192], P('win', 'chan'), may hold values from -600 to 600
- bandpass_taps: bfloat16 [65], replicated, may hold values from -0.75 to 0.75
- pair_offsets: int32 [32, 6], P('chan'), may hold values from -1 to 31, as said below
- lag_limit: int32 [32, 6], P('chan'), may hold values from 1 to 8
Outputs:
- correlations: float32 [6, 8192, 2176], P(None, ('chan', 'win'))
Inputs may be any that keep to these rules, and one draw needn't show every extreme that they name: `pair_offsets`: row b lists distinct block offsets o (partner block (b + o) mod 32) in its first slots and -1 in the remaining slots; every row has at least one offset, some row uses all 6 slots and some row only one.
All inputs are finite; a program needn't handle non-finite values.
Results may differ from a plain program's by a relative error of at most 0.0027.
Values may be sent and summed in bfloat16 or wider, within the bound.
No kernel may reach another device: no remote copies, remote signals or barrier semaphores. Data moves between devices by JAX's collectives and lax.ppermute only.
A program may use at most 128 MiB of HBM per device.

v0:
```python
import math

import jax
import jax.numpy as jnp
from jax import lax
from jax.sharding import PartitionSpec as P


VIRTUAL_SOURCES = 128
MAXIMUM_LAG = 8


def shifted(block, axis, distance):
    devices = range(lax.axis_size(axis))
    route = [(i, (i + distance) % len(devices)) for i in devices]
    return lax.ppermute(block, axis, route)


def band_filter(values, taps):
    samples, channel_count = values.shape
    tap_count = taps.shape[0]
    half_width = (tap_count - 1) // 2
    block_len = min(256, samples)
    pieces = samples // block_len
    padded = jnp.pad(values, ((half_width, half_width), (0, 0)))
    head_rows = padded[:samples].reshape(pieces, block_len, channel_count)
    rest_rows = jnp.pad(padded[block_len:], ((0, block_len - 2 * half_width), (0, 0)))
    tail_rows = rest_rows.reshape(pieces, block_len, channel_count)[:, : 2 * half_width]
    window = jnp.concatenate([head_rows, tail_rows], axis=1)
    period = jnp.concatenate([taps, jnp.zeros((block_len,), taps.dtype)])
    matrix = jnp.tile(period, block_len)[: block_len * (block_len + 2 * half_width)]
    matrix = matrix.reshape(block_len, block_len + 2 * half_width)
    filtered = jnp.einsum("ij,bjc->bic", matrix, window, preferred_element_type=jnp.float32)
    return filtered.reshape(samples, channel_count)


def normalize(window, taps):
    filtered = band_filter(window, taps)
    tap_count = taps.shape[0]
    magnitude = jnp.abs(filtered).astype(jnp.bfloat16)
    box_taps = jnp.ones((tap_count,), jnp.bfloat16)
    mean_level = band_filter(magnitude, box_taps) * (1.0 / tap_count)
    return (filtered / (mean_level + 1e-05)).astype(jnp.bfloat16)


def on_device(strain_rate, bandpass_taps, pair_offsets, lag_limit):
    n_chan = lax.axis_size("chan")
    n_win = lax.axis_size("win")
    _, piece, channels = strain_rate.shape
    channel_count = channels // n_chan
    spacing = channel_count // VIRTUAL_SOURCES
    group = VIRTUAL_SOURCES // n_win
    rows = channel_count // n_win
    lags = 2 * MAXIMUM_LAG + 1

    blocks_first = jnp.transpose(strain_rate[0].reshape(piece, n_chan, channel_count), (1, 0, 2))
    gathered = lax.all_to_all(blocks_first, "chan", 0, 0, tiled=True)
    receivers = normalize(gathered.reshape(n_chan * piece, channel_count), bandpass_taps)
    samples = receivers.shape[0]

    me = lax.axis_index("win")
    pick = (
        jnp.arange(channel_count, dtype=jnp.int32)[None, :]
        == spacing * jnp.arange(VIRTUAL_SOURCES, dtype=jnp.int32)[:, None]
    ).astype(receivers.dtype)
    sources = lax.dot_general(
        pick, receivers, (((1,), (1,)), ((), ())), preferred_element_type=jnp.float32
    ).astype(receivers.dtype).reshape(n_win, group, samples)
    source_pieces = [lax.dynamic_index_in_dim(sources, me, 0, keepdims=False)]
    receiver_pieces = [receivers]
    for distance in range(1, n_win):
        target = lax.rem(me + distance, n_win)
        source_pieces.append(
            shifted(lax.dynamic_index_in_dim(sources, target, 0, keepdims=False), "win", distance)
        )
        receiver_pieces.append(shifted(receivers, "win", distance))
    stack = jnp.stack(receiver_pieces)

    block = lax.axis_index("chan")
    offsets = pair_offsets[0]
    limits = lag_limit[0]
    slots = offsets.shape[0]

    partners = lax.rem(block + offsets + n_chan, n_chan)
    half = n_win // 2
    product = None
    for first in (0, half):
        panels = lax.all_gather(
            jnp.stack(source_pieces[first : first + half]), "chan", axis=0, tiled=False
        )
        if product is not None:
            panels, product = lax.optimization_barrier((panels, product))
        chosen = jnp.take(panels, partners, axis=0, mode="clip")
        padded = jnp.pad(chosen, ((0, 0), (0, 0), (0, 0), (MAXIMUM_LAG, MAXIMUM_LAG)))
        columns = []
        for w in range(half):
            lag_rows = jnp.stack([padded[:, w, :, i : i + samples] for i in range(lags)], axis=1)
            columns.append(lag_rows.reshape(slots * lags * group, samples))
        lagged = jnp.concatenate(columns, axis=1)
        partial = lax.dot_general(
            lagged,
            stack[first : first + half].reshape(half * samples, channel_count),
            (((1,), (0,)), ((), ())),
            preferred_element_type=jnp.float32,
        )
        product = partial if product is None else product + partial
    lag_ids = jnp.arange(lags, dtype=jnp.int32) - MAXIMUM_LAG
    kept = (jnp.abs(lag_ids)[None, :] <= limits[:, None]) & (offsets >= 0)[:, None]
    factor = 1.0 / math.sqrt(samples * n_win)
    weights = jnp.repeat(kept.astype(jnp.float32).reshape(slots * lags), group) * factor
    result = jnp.transpose(product * weights[:, None]).reshape(n_win, rows, slots * lags * group)
    result = lax.all_to_all(result, "win", 0, 0, tiled=True)
    result = result.reshape(n_win, rows, slots, lags, group)
    result = jnp.transpose(result, (2, 1, 3, 0, 4))
    return result.reshape(slots, rows, lags * VIRTUAL_SOURCES)


def solution(mesh):
    placed = (P("win", "chan", None), P(), P("chan", None), P("chan", None))
    return jax.shard_map(
        on_device,
        mesh=mesh,
        in_specs=placed,
        out_specs=P(None, ("chan", "win"), None),
        check_vma=False,
    )
```

profile of v0, /device:TPU:33, one launch (start us, length us, event | category | flops | bytes accessed | tf_op | source)
XLA Modules:
  0.0 254.3 jit_solution(4191981502098957714)
XLA Ops:
  8.8 9.9 %all-to-all-start = ((bf16[32,32,256]{2,1,0:T(8,128)(2,1)}), bf16[32,32,256]{2,1,0:T(8,128)(2,1)S(1)}, u32[]{:S(2)}, u32[]{:S(2)}) async-start(bf16[32,32,256]{2,1,0:T(8,128)(2,1)} %copy.26), calls=%async_computation | async-start | bytes 1048576 | tf_op jit(solution)/shard_map/all_to_all | solution.py:57
  21.0 14.1 %all-to-all-done = bf16[32,32,256]{2,1,0:T(8,128)(2,1)S(1)} async-done(((bf16[32,32,256]{2,1,0:T(8,128)(2,1)}), bf16[32,32,256]{2,1,0:T(8,128)(2,1)S(1)}, u32[]{:S(2)}, u32[]{:S(2)}) %all-to-all-start) | async-done | bytes 524320 | tf_op jit(solution)/shard_map/all_to_all | solution.py:57
  38.1 2.6 %collective-permute-start.5 = (bf16[16,1024]{1,0:T(8,128)(2,1)S(1)}, bf16[16,1024]{1,0:T(8,128)(2,1)S(1)}, u32[]{:S(2)}, u32[]{:S(2)}) collective-permute-start(bf16[16,1024]{1,0:T(8,128)(2,1)S(1)} %get-tuple-element.29), channel_id=1, source_target_pairs={{0,2},{1,3},{2,4},{3,5},{4,6},{5,7},{6,0},{7,1},{8,10},{9,11},{10,... | collective-permute-start | bytes 98312 | tf_op jit(solution)/shard_map/ppermute | solution.py:16
  40.7 3.2 %collective-permute-start.6 = (bf16[16,1024]{1,0:T(8,128)(2,1)S(1)}, bf16[16,1024]{1,0:T(8,128)(2,1)S(1)}, u32[]{:S(2)}, u32[]{:S(2)}) collective-permute-start(bf16[16,1024]{1,0:T(8,128)(2,1)S(1)} %get-tuple-element.28), channel_id=1, source_target_pairs={{0,3},{1,4},{2,5},{3,6},{4,7},{5,0},{6,1},{7,2},{8,11},{9,12},{10,... | collective-permute-start | bytes 98312 | tf_op jit(solution)/shard_map/ppermute | solution.py:16
  50.5 4.7 %collective-permute-start.1 = (bf16[16,1024]{1,0:T(8,128)(2,1)S(1)}, bf16[16,1024]{1,0:T(8,128)(2,1)S(1)}, u32[]{:S(2)}, u32[]{:S(2)}) collective-permute-start(bf16[16,1024]{1,0:T(8,128)(2,1)S(1)} %get-tuple-element.33), channel_id=1, source_target_pairs={{0,5},{1,6},{2,7},{3,0},{4,1},{5,2},{6,3},{7,4},{8,13},{9,14},{10,... | collective-permute-start | bytes 98312 | tf_op jit(solution)/shard_map/ppermute | solution.py:16
  55.2 15.8 %collective-permute-start.2 = (bf16[16,1024]{1,0:T(8,128)(2,1)S(1)}, bf16[16,1024]{1,0:T(8,128)(2,1)S(1)}, u32[]{:S(2)}, u32[]{:S(2)}) collective-permute-start(bf16[16,1024]{1,0:T(8,128)(2,1)S(1)} %get-tuple-element.32), channel_id=1, source_target_pairs={{0,6},{1,7},{2,0},{3,1},{4,2},{5,3},{6,4},{7,5},{8,14},{9,15},{10,... | collective-permute-start | bytes 98312 | tf_op jit(solution)/shard_map/ppermute | solution.py:16
  71.0 5.8 %collective-permute-done.1 = bf16[16,1024]{1,0:T(8,128)(2,1)S(1)} collective-permute-done((bf16[16,1024]{1,0:T(8,128)(2,1)S(1)}, bf16[16,1024]{1,0:T(8,128)(2,1)S(1)}, u32[]{:S(2)}, u32[]{:S(2)}) %collective-permute-start.1) | collective-permute-done | bytes 32800 | tf_op jit(solution)/shard_map/ppermute | solution.py:16
  76.8 11.9 %collective-permute-start.3 = (bf16[16,1024]{1,0:T(8,128)(2,1)S(1)}, bf16[16,1024]{1,0:T(8,128)(2,1)S(1)}, u32[]{:S(2)}, u32[]{:S(2)}) collective-permute-start(bf16[16,1024]{1,0:T(8,128)(2,1)S(1)} %get-tuple-element.31), channel_id=1, source_target_pairs={{0,7},{1,0},{2,1},{3,2},{4,3},{5,4},{6,5},{7,6},{8,15},{9,8},{10,9... | collective-permute-start | bytes 98312 | tf_op jit(solution)/shard_map/ppermute | solution.py:16
  88.8 2.1 collective-permute-done.3
  91.0 9.6 %collective-permute-start.11 = (bf16[1024,256]{1,0:T(8,128)(2,1)S(1)}, bf16[1024,256]{1,0:T(8,128)(2,1)S(1)}, u32[]{:S(2)}, u32[]{:S(2)}) collective-permute-start(bf16[1024,256]{1,0:T(8,128)(2,1)S(1)} %bitcast.100), channel_id=1, source_target_pairs={{0,5},{1,6},{2,7},{3,0},{4,1},{5,2},{6,3},{7,4},{8,13},{9,14},{10,... | collective-permute-start | bytes 1572872 | tf_op jit(solution)/shard_map/ppermute | solution.py:16
  100.6 3.3 %collective-permute-start.12 = (bf16[1024,256]{1,0:T(8,128)(2,1)S(1)}, bf16[1024,256]{1,0:T(8,128)(2,1)}, u32[]{:S(2)}, u32[]{:S(2)}) collective-permute-start(bf16[1024,256]{1,0:T(8,128)(2,1)S(1)} %bitcast.101), channel_id=1, source_target_pairs={{0,6},{1,7},{2,0},{3,1},{4,2},{5,3},{6,4},{7,5},{8,14},{9,15},{10,... | collective-permute-start | bytes 1572872 | tf_op jit(solution)/shard_map/ppermute | solution.py:16
  106.5 5.4 %collective-permute-done.11 = bf16[1024,256]{1,0:T(8,128)(2,1)S(1)} collective-permute-done((bf16[1024,256]{1,0:T(8,128)(2,1)S(1)}, bf16[1024,256]{1,0:T(8,128)(2,1)S(1)}, u32[]{:S(2)}, u32[]{:S(2)}) %collective-permute-start.11) | collective-permute-done | bytes 524320 | tf_op jit(solution)/shard_map/ppermute | solution.py:16
  112.0 14.0 %collective-permute-done.12 = bf16[1024,256]{1,0:T(8,128)(2,1)} collective-permute-done((bf16[1024,256]{1,0:T(8,128)(2,1)S(1)}, bf16[1024,256]{1,0:T(8,128)(2,1)}, u32[]{:S(2)}, u32[]{:S(2)}) %collective-permute-start.12) | collective-permute-done | bytes 524320 | tf_op jit(solution)/shard_map/ppermute | solution.py:16
  126.0 16.3 %collective-permute-done.13 = bf16[1024,256]{1,0:T(8,128)(2,1)} collective-permute-done((bf16[1024,256]{1,0:T(8,128)(2,1)S(1)}, bf16[1024,256]{1,0:T(8,128)(2,1)}, u32[]{:S(2)}, u32[]{:S(2)}) %collective-permute-start.13) | collective-permute-done | bytes 524320 | tf_op jit(solution)/shard_map/ppermute | solution.py:16
  143.8 2.8 %gather_fusion = bf16[6,4,16,1024]{3,2,1,0:T(8,128)(2,1)S(1)} fusion(bf16[32,4,16,1024]{3,2,1,0:T(8,128)(2,1)} %bitcast.115, s32[1024]{0:T(1024)S(1)} %pad_clamp_fusion), kind=kCustom, calls=%fused_computation | custom fusion | bytes 1572888 | tf_op jit(solution)/shard_map/jit(_take)/gather | solution.py:93
  156.9 7.1 %fusion = f32[1632,256]{1,0:T(8,128)} fusion(bf16[4096,256]{1,0:T(8,128)(2,1)S(1)} %bitcast.93, bf16[1632,1024]{1,0:T(8,128)(2,1)S(1)} %bitcast.124, bf16[1632,1024]{1,0:T(8,128)(2,1)S(1)} %bitcast.123, bf16[1632,1024]{1,0:T(8,128)(2,1)} %bitcast.127, bf16[1632,1024]{1,0:T(8,128)(2,1)} %bitcast.129), kind=kOutput, calls=%fused_computation.2 | convolution fusion | flops 3476029440 | bytes 17137664 | tf_op jit(solution)/shard_map/dot_general | solution.py:100
  164.0 13.9 %all-gather.5.cloned.1.call-done = bf16[128,16,1024]{2,1,0:T(8,128)(2,1)} async-done(((bf16[4,16,1024]{2,1,0:T(8,128)(2,1)}), bf16[128,16,1024]{2,1,0:T(8,128)(2,1)}) %all-gather.5.cloned.1.call-update) | async-done | bytes 4194320 | tf_op jit(solution)/shard_map/all_gather | solution.py:88
  177.9 2.8 %gather_fusion.1 = bf16[6,4,16,1024]{3,2,1,0:T(8,128)(2,1)S(1)} fusion(bf16[32,4,16,1024]{3,2,1,0:T(8,128)(2,1)} %bitcast.114, s32[1024]{0:T(1024)S(1)} %pad_clamp_fusion), kind=kCustom, calls=%fused_computation.1 | custom fusion | bytes 1572888 | tf_op jit(solution)/shard_map/jit(_take)/gather | solution.py:93
  192.0 7.5 %fusion.22 = f32[256,1632]{0,1:T(8,128)} fusion(f32[1632,256]{1,0:T(8,128)S(1)} %copy-done.9, bf16[4096,256]{1,0:T(8,128)(2,1)S(1)} %bitcast.92, bf16[1632,1024]{1,0:T(8,128)(2,1)} %bitcast.126, bf16[1632,1024]{1,0:T(8,128)(2,1)S(1)} %bitcast.125, bf16[1632,1024]{1,0:T(8,128)(2,1)} %bitcast.128, bf16[1632,1024]{1,0:T(8,128)(2,1)} %bitcast.130, ...), kind=kOutput, calls=%fused_computation.20 | convolution fusion | flops 3476865024 | bytes 18815360 | tf_op jit(solution)/shard_map/dot_general | solution.py:100
  199.5 1.8 copy.29
  201.3 29.4 %all_to_all.10 = f32[8,32,1632]{2,1,0:T(8,128)S(1)} all-to-all(f32[8,32,1632]{2,1,0:T(8,128)S(1)} %bitcast.86), channel_id=1, replica_groups=mesh['chan'=32,'win'=8] {'win'}, dimensions={0} | all-to-all | bytes 3342336 | tf_op jit(solution)/shard_map/all_to_all | solution.py:112
  230.7 4.3 %copy.30 = f32[8,32,1632]{1,2,0:T(8,128)} copy(f32[8,32,1632]{2,1,0:T(8,128)S(1)} %all_to_all.10) | data formatting | bytes 3342336 | tf_op jit(solution)/shard_map/all_to_all | solution.py:112
  235.0 6.8 %copy.31 = f32[6,32,17,8,16]{1,4,3,2,0:T(8,128)} copy(f32[6,32,17,8,16]{1,4,2,0,3:T(8,128)} %bitcast.84) | data formatting | bytes 3342336 | tf_op jit(solution)/shard_map/transpose | solution.py:114
  241.8 5.7 %copy.32 = f32[6,32,2176]{2,1,0:T(8,128)} copy(f32[6,32,2176]{1,2,0:T(8,128)} %bitcast.85) | data formatting | bytes 3342336 | tf_op jit(solution)/shard_map/reshape | solution.py:115
  (201 shorter events, 38.6 us)
Async XLA Ops:
  6.5 13.7 %copy-start.6 = (bf16[321]{0:T(512)(128)(2,1)S(1)}, bf16[321]{0:T(512)(128)(2,1)}, u32[]{:S(2)}) copy-start(bf16[321]{0:T(512)(128)(2,1)} %constant.64.clone.1) | copy-start | bytes 1930
  8.8 26.4 %all-to-all-start = ((bf16[32,32,256]{2,1,0:T(8,128)(2,1)}), bf16[32,32,256]{2,1,0:T(8,128)(2,1)S(1)}, u32[]{:S(2)}, u32[]{:S(2)}) async-start(bf16[32,32,256]{2,1,0:T(8,128)(2,1)} %copy.26), calls=%async_computation | async-start | bytes 1048576 | tf_op jit(solution)/shard_map/all_to_all | solution.py:57
  18.7 125.0 %all-gather.7.cloned.1.call-start = ((), (), s32[]{:S(2)}) async-start(), calls=%async_computation.3 | async-start | bytes 4325376 | tf_op jit(solution)/shard_map/all_gather | solution.py:88
  35.9 14.1 %copy-start.8 = (s32[1,6]{1,0:T(1,128)S(1)}, s32[1,6]{1,0:T(1,128)}, u32[]{:S(2)}) copy-start(s32[1,6]{1,0:T(1,128)} %param.6) | copy-start | bytes 76
  35.9 52.8 %copy-start.7 = (s32[1,6]{1,0:T(1,128)S(1)}, s32[1,6]{1,0:T(1,128)}, u32[]{:S(2)}) copy-start(s32[1,6]{1,0:T(1,128)} %param.7) | copy-start | bytes 76
  36.7 7.2 %collective-permute-start.4 = (bf16[16,1024]{1,0:T(8,128)(2,1)S(1)}, bf16[16,1024]{1,0:T(8,128)(2,1)S(1)}, u32[]{:S(2)}, u32[]{:S(2)}) collective-permute-start(bf16[16,1024]{1,0:T(8,128)(2,1)S(1)} %get-tuple-element.30), channel_id=1, source_target_pairs={{0,1},{1,2},{2,3},{3,4},{4,5},{5,6},{6,7},{7,0},{8,9},{9,10},{10,1... | collective-permute-start | bytes 98312 | tf_op jit(solution)/shard_map/ppermute | solution.py:16
  38.1 6.7 %collective-permute-start.5 = (bf16[16,1024]{1,0:T(8,128)(2,1)S(1)}, bf16[16,1024]{1,0:T(8,128)(2,1)S(1)}, u32[]{:S(2)}, u32[]{:S(2)}) collective-permute-start(bf16[16,1024]{1,0:T(8,128)(2,1)S(1)} %get-tuple-element.29), channel_id=1, source_target_pairs={{0,2},{1,3},{2,4},{3,5},{4,6},{5,7},{6,0},{7,1},{8,10},{9,11},{10,... | collective-permute-start | bytes 98312 | tf_op jit(solution)/shard_map/ppermute | solution.py:16
  40.7 5.5 %collective-permute-start.6 = (bf16[16,1024]{1,0:T(8,128)(2,1)S(1)}, bf16[16,1024]{1,0:T(8,128)(2,1)S(1)}, u32[]{:S(2)}, u32[]{:S(2)}) collective-permute-start(bf16[16,1024]{1,0:T(8,128)(2,1)S(1)} %get-tuple-element.28), channel_id=1, source_target_pairs={{0,3},{1,4},{2,5},{3,6},{4,7},{5,0},{6,1},{7,2},{8,11},{9,12},{10,... | collective-permute-start | bytes 98312 | tf_op jit(solution)/shard_map/ppermute | solution.py:16
  46.9 131.0 %all-gather.5.cloned.1.call-start = ((), (), s32[]{:S(2)}) async-start(), calls=%async_computation.2 | async-start | bytes 4325376 | tf_op jit(solution)/shard_map/all_gather | solution.py:88
  47.0 53.6 %collective-permute-start.7 = (bf16[1024,256]{1,0:T(8,128)(2,1)S(1)}, bf16[1024,256]{1,0:T(8,128)(2,1)S(1)}, u32[]{:S(2)}, u32[]{:S(2)}) collective-permute-start(bf16[1024,256]{1,0:T(8,128)(2,1)S(1)} %bitcast.96), channel_id=1, source_target_pairs={{0,1},{1,2},{2,3},{3,4},{4,5},{5,6},{6,7},{7,0},{8,9},{9,10},{10,1... | collective-permute-start | bytes 1572872 | tf_op jit(solution)/shard_map/ppermute | solution.py:16
  48.5 55.3 %collective-permute-start.8 = (bf16[1024,256]{1,0:T(8,128)(2,1)S(1)}, bf16[1024,256]{1,0:T(8,128)(2,1)S(1)}, u32[]{:S(2)}, u32[]{:S(2)}) collective-permute-start(bf16[1024,256]{1,0:T(8,128)(2,1)S(1)} %bitcast.97), channel_id=1, source_target_pairs={{0,2},{1,3},{2,4},{3,5},{4,6},{5,7},{6,0},{7,1},{8,10},{9,11},{10,... | collective-permute-start | bytes 1572872 | tf_op jit(solution)/shard_map/ppermute | solution.py:16
  50.0 5.2 %collective-permute-start = (bf16[16,1024]{1,0:T(8,128)(2,1)S(1)}, bf16[16,1024]{1,0:T(8,128)(2,1)S(1)}, u32[]{:S(2)}, u32[]{:S(2)}) collective-permute-start(bf16[16,1024]{1,0:T(8,128)(2,1)S(1)} %get-tuple-element.34), channel_id=1, source_target_pairs={{0,4},{1,5},{2,6},{3,7},{4,0},{5,1},{6,2},{7,3},{8,12},{9,13},{10,... | collective-permute-start | bytes 98312 | tf_op jit(solution)/shard_map/ppermute | solution.py:16
  50.5 26.3 %collective-permute-start.1 = (bf16[16,1024]{1,0:T(8,128)(2,1)S(1)}, bf16[16,1024]{1,0:T(8,128)(2,1)S(1)}, u32[]{:S(2)}, u32[]{:S(2)}) collective-permute-start(bf16[16,1024]{1,0:T(8,128)(2,1)S(1)} %get-tuple-element.33), channel_id=1, source_target_pairs={{0,5},{1,6},{2,7},{3,0},{4,1},{5,2},{6,3},{7,4},{8,13},{9,14},{10,... | collective-permute-start | bytes 98312 | tf_op jit(solution)/shard_map/ppermute | solution.py:16
  55.2 49.7 %collective-permute-start.9 = (bf16[1024,256]{1,0:T(8,128)(2,1)S(1)}, bf16[1024,256]{1,0:T(8,128)(2,1)S(1)}, u32[]{:S(2)}, u32[]{:S(2)}) collective-permute-start(bf16[1024,256]{1,0:T(8,128)(2,1)S(1)} %bitcast.98), channel_id=1, source_target_pairs={{0,3},{1,4},{2,5},{3,6},{4,7},{5,0},{6,1},{7,2},{8,11},{9,12},{10,... | collective-permute-start | bytes 1572872 | tf_op jit(solution)/shard_map/ppermute | solution.py:16
  55.2 33.6 %collective-permute-start.2 = (bf16[16,1024]{1,0:T(8,128)(2,1)S(1)}, bf16[16,1024]{1,0:T(8,128)(2,1)S(1)}, u32[]{:S(2)}, u32[]{:S(2)}) collective-permute-start(bf16[16,1024]{1,0:T(8,128)(2,1)S(1)} %get-tuple-element.32), channel_id=1, source_target_pairs={{0,6},{1,7},{2,0},{3,1},{4,2},{5,3},{6,4},{7,5},{8,14},{9,15},{10,... | collective-permute-start | bytes 98312 | tf_op jit(solution)/shard_map/ppermute | solution.py:16
  76.8 14.2 %collective-permute-start.3 = (bf16[16,1024]{1,0:T(8,128)(2,1)S(1)}, bf16[16,1024]{1,0:T(8,128)(2,1)S(1)}, u32[]{:S(2)}, u32[]{:S(2)}) collective-permute-start(bf16[16,1024]{1,0:T(8,128)(2,1)S(1)} %get-tuple-element.31), channel_id=1, source_target_pairs={{0,7},{1,0},{2,1},{3,2},{4,3},{5,4},{6,5},{7,6},{8,15},{9,8},{10,9... | collective-permute-start | bytes 98312 | tf_op jit(solution)/shard_map/ppermute | solution.py:16
  88.8 17.8 %collective-permute-start.10 = (bf16[1024,256]{1,0:T(8,128)(2,1)S(1)}, bf16[1024,256]{1,0:T(8,128)(2,1)S(1)}, u32[]{:S(2)}, u32[]{:S(2)}) collective-permute-start(bf16[1024,256]{1,0:T(8,128)(2,1)S(1)} %bitcast.99), channel_id=1, source_target_pairs={{0,4},{1,5},{2,6},{3,7},{4,0},{5,1},{6,2},{7,3},{8,12},{9,13},{10,... | collective-permute-start | bytes 1572872 | tf_op jit(solution)/shard_map/ppermute | solution.py:16
  91.0 21.0 %collective-permute-start.11 = (bf16[1024,256]{1,0:T(8,128)(2,1)S(1)}, bf16[1024,256]{1,0:T(8,128)(2,1)S(1)}, u32[]{:S(2)}, u32[]{:S(2)}) collective-permute-start(bf16[1024,256]{1,0:T(8,128)(2,1)S(1)} %bitcast.100), channel_id=1, source_target_pairs={{0,5},{1,6},{2,7},{3,0},{4,1},{5,2},{6,3},{7,4},{8,13},{9,14},{10,... | collective-permute-start | bytes 1572872 | tf_op jit(solution)/shard_map/ppermute | solution.py:16
  100.6 25.5 %collective-permute-start.12 = (bf16[1024,256]{1,0:T(8,128)(2,1)S(1)}, bf16[1024,256]{1,0:T(8,128)(2,1)}, u32[]{:S(2)}, u32[]{:S(2)}) collective-permute-start(bf16[1024,256]{1,0:T(8,128)(2,1)S(1)} %bitcast.101), channel_id=1, source_target_pairs={{0,6},{1,7},{2,0},{3,1},{4,2},{5,3},{6,4},{7,5},{8,14},{9,15},{10,... | collective-permute-start | bytes 1572872 | tf_op jit(solution)/shard_map/ppermute | solution.py:16
  103.9 38.4 %collective-permute-start.13 = (bf16[1024,256]{1,0:T(8,128)(2,1)S(1)}, bf16[1024,256]{1,0:T(8,128)(2,1)}, u32[]{:S(2)}, u32[]{:S(2)}) collective-permute-start(bf16[1024,256]{1,0:T(8,128)(2,1)S(1)} %bitcast.102), channel_id=1, source_target_pairs={{0,7},{1,0},{2,1},{3,2},{4,3},{5,4},{6,5},{7,6},{8,15},{9,8},{10,9... | collective-permute-start | bytes 1572872 | tf_op jit(solution)/shard_map/ppermute | solution.py:16
  148.9 1.8 copy-start.4
  183.0 1.8 copy-start.5
  185.9 1.7 copy-start.3
  189.4 2.6 %copy-start.9 = (f32[1632,256]{1,0:T(8,128)S(1)}, f32[1632,256]{1,0:T(8,128)}, u32[]{:S(2)}) copy-start(f32[1632,256]{1,0:T(8,128)} %fusion) | copy-start | bytes 5013508
  (3 other events, 5.0 us)
Sparse Core Ops, SparseCore 0:
  47.0 62.8 all-gather.6
  111.8 66.1 all-gather.4
where the time goes:
time: 256 us; the launch traced here: 254 us
  waiting for transfers between devices  74 us (29%)
  starting transfers between devices  66.2 us (26%)
  local copies, waits for them, and re-layouts  49.7 us (19%)
  blocking collectives  29.4 us (11%)
  matrix products  15.8 us (6%)
  between operations  14.7 us (6%)
  other arithmetic  4.6 us (2%)
    ppermute x14, starting transfers between devices, shifted(): return lax.ppermute(block, axis, route)  56.1 us
    ppermute x14, waiting for transfers between devices, shifted(): return lax.ppermute(block, axis, route)  45.9 us
    all_to_all x1, blocking collectives, on_device(): result = lax.all_to_all(result, 'win', 0, 0, tiled=True)  29.4 us
    unnamed x137, local copies, waits for them, and re-layouts  20.1 us
    dot_general x2, matrix products, on_device(): lax.dot_general(lagged, stack[first:first + half].reshape(half * samples,...  14.6 us
    all_to_all x1, waiting for transfers between devices, on_device(): gathered = lax.all_to_all(blocks_first, 'chan', 0, 0, tiled=True)  14.1 us
    all_gather x2, waiting for transfers between devices, on_device(): lax.all_gather(jnp.stack(source_pieces[first:first + half]), 'chan', axis...  14 us
    all_to_all x1, starting transfers between devices, on_device(): gathered = lax.all_to_all(blocks_first, 'chan', 0, 0, tiled=True)  9.94 us
  transfers between devices with their start and end apart: 17, of which 9 were waited for; matrix products, arithmetic and copies ran while one was open for 9% of the time, Pallas kernels for 0%

commit v1 on v0

--- a/solution.py
+++ b/solution.py
@@ -3,7 +3,7 @@
 import jax
 import jax.numpy as jnp
 from jax import lax
-from jax.sharding import PartitionSpec as P
+from jax.sharding import Mesh, PartitionSpec as P
 
 
 VIRTUAL_SOURCES = 128
@@ -44,7 +44,10 @@
 
 
 def on_device(strain_rate, bandpass_taps, pair_offsets, lag_limit):
-    n_chan = lax.axis_size("chan")
+    blocks_axis = ("chips", "core")
+    n_chips = lax.axis_size("chips")
+    n_core = lax.axis_size("core")
+    n_chan = n_chips * n_core
     n_win = lax.axis_size("win")
     _, piece, channels = strain_rate.shape
     channel_count = channels // n_chan
@@ -54,7 +57,7 @@
     lags = 2 * MAXIMUM_LAG + 1
 
     blocks_first = jnp.transpose(strain_rate[0].reshape(piece, n_chan, channel_count), (1, 0, 2))
-    gathered = lax.all_to_all(blocks_first, "chan", 0, 0, tiled=True)
+    gathered = lax.all_to_all(blocks_first, blocks_axis, 0, 0, tiled=True)
     receivers = normalize(gathered.reshape(n_chan * piece, channel_count), bandpass_taps)
     samples = receivers.shape[0]
 
@@ -75,19 +78,28 @@
         )
         receiver_pieces.append(shifted(receivers, "win", distance))
     stack = jnp.stack(receiver_pieces)
+    panel = jnp.stack(source_pieces)
 
-    block = lax.axis_index("chan")
+    core = lax.axis_index("core")
+    half = n_win // n_core
+    share = panel.reshape(n_core, half, group, samples)
+    mine = lax.dynamic_index_in_dim(share, core, 0, keepdims=False)
+    other = lax.dynamic_index_in_dim(share, 1 - core, 0, keepdims=False)
+    sibling = lax.ppermute(other, "core", [(0, 1), (1, 0)])
+    first_is_mine = core == 0
+    pair = jnp.stack([jnp.where(first_is_mine, mine, sibling), jnp.where(first_is_mine, sibling, mine)])
+    own_half = lax.all_gather(pair, "chips", axis=0, tiled=True).reshape(n_chan, half, group, samples)
+    other_half = lax.ppermute(own_half, "core", [(0, 1), (1, 0)])
+
+    block = lax.axis_index("chips") * n_core + core
     offsets = pair_offsets[0]
     limits = lag_limit[0]
     slots = offsets.shape[0]
+    partners = lax.rem(block + offsets + n_chan, n_chan)
+    stack = stack.reshape(n_core, half, samples, channel_count)
 
-    partners = lax.rem(block + offsets + n_chan, n_chan)
-    half = n_win // 2
     product = None
-    for first in (0, half):
-        panels = lax.all_gather(
-            jnp.stack(source_pieces[first : first + half]), "chan", axis=0, tiled=False
-        )
+    for panels, which in ((own_half, core), (other_half, 1 - core)):
         if product is not None:
             panels, product = lax.optimization_barrier((panels, product))
         chosen = jnp.take(panels, partners, axis=0, mode="clip")
@@ -99,7 +111,9 @@
         lagged = jnp.concatenate(columns, axis=1)
         partial = lax.dot_general(
             lagged,
-            stack[first : first + half].reshape(half * samples, channel_count),
+            lax.dynamic_index_in_dim(stack, which, 0, keepdims=False).reshape(
+                half * samples, channel_count
+            ),
             (((1,), (0,)), ((), ())),
             preferred_element_type=jnp.float32,
         )
@@ -116,11 +130,16 @@
 
 
 def solution(mesh):
-    placed = (P("win", "chan", None), P(), P("chan", None), P("chan", None))
+    chan_size = mesh.shape["chan"]
+    by_chip = Mesh(
+        mesh.devices.reshape(chan_size // 2, 2, mesh.shape["win"]), ("chips", "core", "win")
+    )
+    blocks_axis = ("chips", "core")
+    placed = (P("win", blocks_axis, None), P(), P(blocks_axis, None), P(blocks_axis, None))
     return jax.shard_map(
         on_device,
-        mesh=mesh,
+        mesh=by_chip,
         in_specs=placed,
-        out_specs=P(None, ("chan", "win"), None),
+        out_specs=P(None, ("chips", "core", "win"), None),
         check_vma=False,
     )

time: 256 us -> 303 us (1.18)
  waiting for transfers between devices: 74 us -> 112 us
  local copies, waits for them, and re-layouts: 49.7 us -> 53.3 us
  other arithmetic: 4.6 us -> 1.21 us
    ppermute x14, waiting for transfers between devices: 45.9 us -> 97.1 us  [shifted(): return lax.ppermute(block, axis, route)]
    all_gather x2 -> x1, waiting for transfers between devices: 14 us -> 0.11 us  [on_device(): lax.all_gather(pair, 'chips', axis=0, tiled=True)]
    ppermute x0 -> x2, starting transfers between devices: none -> 4.94 us  [the longest x1 3.66 us: on_device(): sibling = lax.ppermute(other, 'core', [(0, 1), (1, 0)])]
    another operation x4 -> x2, other arithmetic: 4.5 us -> 0.75 us  [on_device(): jnp.stack([jnp.where(first_is_mine, mine, sibling), jnp.where(first_is_mi...]
    unnamed x137 -> x156, local copies, waits for them, and re-layouts: 20.1 us -> 23.1 us
  transfers between devices with their start and end apart: 17 -> 18, of which waited for: 9 -> 10; matrix products, arithmetic and copies ran while one was open for 9% -> 5% of each run, Pallas kernels for 0% -> 0%
where the time goes in v1:
time: 303 us; the launch traced here: 299 us
  waiting for transfers between devices  112 us (37%)
  starting transfers between devices  68.9 us (23%)
  local copies, waits for them, and re-layouts  53.3 us (18%)
  blocking collectives  32.4 us (11%)
  matrix products  16.5 us (5%)
  between operations  14.8 us (5%)
    ppermute x14, waiting for transfers between devices, shifted(): return lax.ppermute(block, axis, route)  97.1 us
    ppermute x14, starting transfers between devices, shifted(): return lax.ppermute(block, axis, route)  54 us
    all_to_all x1, blocking collectives, on_device(): result = lax.all_to_all(result, 'win', 0, 0, tiled=True)  32.4 us
    unnamed x156, local copies, waits for them, and re-layouts  23.1 us
    dot_general x2, matrix products, on_device(): lax.dot_general(lagged, lax.dynamic_index_in_dim(stack, which, 0, keepdim...  15.3 us
    all_to_all x1, waiting for transfers between devices, on_device(): gathered = lax.all_to_all(blocks_first, blocks_axis, 0, 0, tiled=True)  14.1 us
    all_to_all x1, starting transfers between devices, on_device(): gathered = lax.all_to_all(blocks_first, blocks_axis, 0, 0, tiled=True)  9.94 us
    transpose x1, local copies, waits for them, and re-layouts, on_device(): result = jnp.transpose(result, (2, 1, 3, 0, 4))  6.76 us
  transfers between devices with their start and end apart: 18, of which 10 were waited for; matrix products, arithmetic and copies ran while one was open for 5% of the time, Pallas kernels for 0%

profile of v1, /device:TPU:33, one launch (start us, length us, event | category | flops | bytes accessed | tf_op | source)
XLA Modules:
  0.0 299.5 jit_solution(7651340598720362129)
XLA Ops:
  8.8 9.9 %all-to-all-start = ((bf16[32,32,256]{2,1,0:T(8,128)(2,1)}), bf16[32,32,256]{2,1,0:T(8,128)(2,1)S(1)}, u32[]{:S(2)}, u32[]{:S(2)}) async-start(bf16[32,32,256]{2,1,0:T(8,128)(2,1)} %copy.26), calls=%async_computation | async-start | bytes 1048576 | tf_op jit(solution)/shard_map/all_to_all | solution.py:60
  21.0 14.1 %all-to-all-done = bf16[32,32,256]{2,1,0:T(8,128)(2,1)S(1)} async-done(((bf16[32,32,256]{2,1,0:T(8,128)(2,1)}), bf16[32,32,256]{2,1,0:T(8,128)(2,1)S(1)}, u32[]{:S(2)}, u32[]{:S(2)}) %all-to-all-start) | async-done | bytes 524320 | tf_op jit(solution)/shard_map/all_to_all | solution.py:60
  38.1 2.6 collective-permute-start.1
  40.8 3.2 %collective-permute-start.2 = (bf16[16,1024]{1,0:T(8,128)(2,1)S(1)}, bf16[16,1024]{1,0:T(8,128)(2,1)S(1)}, u32[]{:S(2)}, u32[]{:S(2)}) collective-permute-start(bf16[16,1024]{1,0:T(8,128)(2,1)S(1)} %get-tuple-element.35), channel_id=1, source_target_pairs={{0,3},{1,4},{2,5},{3,6},{4,7},{5,0},{6,1},{7,2},{8,11},{9,12},{10,... | collective-permute-start | bytes 98312 | tf_op jit(solution)/shard_map/ppermute | solution.py:16
  44.5 2.6 collective-permute-start.4
  47.1 2.7 collective-permute-start.5
  52.6 3.7 %collective-permute-start.7 = (bf16[4,16,1024]{2,1,0:T(8,128)(2,1)S(1)}, bf16[4,16,1024]{2,1,0:T(8,128)(2,1)S(1)}, u32[]{:S(2)}, u32[]{:S(2)}) collective-permute-start(bf16[4,16,1024]{2,1,0:T(8,128)(2,1)S(1)} %dynamic-slice_bitcast_fusion), channel_id=1, source_target_pairs={{0,8},{8,0},{1,9},{9,1},{2,10},{10,2},{3,11},{11,3},{4,12},{12,4},... | collective-permute-start | bytes 393224 | tf_op jit(solution)/shard_map/ppermute | solution.py:88
  58.3 3.9 %collective-permute-start.10 = (bf16[1024,256]{1,0:T(8,128)(2,1)S(1)}, bf16[1024,256]{1,0:T(8,128)(2,1)S(1)}, u32[]{:S(2)}, u32[]{:S(2)}) collective-permute-start(bf16[1024,256]{1,0:T(8,128)(2,1)S(1)} %bitcast.124), channel_id=1, source_target_pairs={{0,2},{1,3},{2,4},{3,5},{4,6},{5,7},{6,0},{7,1},{8,10},{9,11},{10,... | collective-permute-start | bytes 1572872 | tf_op jit(solution)/shard_map/ppermute | solution.py:16
  62.5 1.8 collective-permute-start.11
  65.3 3.6 %collective-permute-start.13 = (bf16[1024,256]{1,0:T(8,128)(2,1)S(1)}, bf16[1024,256]{1,0:T(8,128)(2,1)S(1)}, u32[]{:S(2)}, u32[]{:S(2)}) collective-permute-start(bf16[1024,256]{1,0:T(8,128)(2,1)S(1)} %bitcast.127), channel_id=1, source_target_pairs={{0,5},{1,6},{2,7},{3,0},{4,1},{5,2},{6,3},{7,4},{8,13},{9,14},{10,... | collective-permute-start | bytes 1572872 | tf_op jit(solution)/shard_map/ppermute | solution.py:16
  69.0 16.5 %collective-permute-done.9 = bf16[1024,256]{1,0:T(8,128)(2,1)S(1)} collective-permute-done((bf16[1024,256]{1,0:T(8,128)(2,1)S(1)}, bf16[1024,256]{1,0:T(8,128)(2,1)S(1)}, u32[]{:S(2)}, u32[]{:S(2)}) %collective-permute-start.9) | collective-permute-done | bytes 524320 | tf_op jit(solution)/shard_map/ppermute | solution.py:16
  86.3 2.7 collective-permute-done.10
  89.0 28.3 %collective-permute-start.15 = (bf16[1024,256]{1,0:T(8,128)(2,1)S(1)}, bf16[1024,256]{1,0:T(8,128)(2,1)S(1)}, u32[]{:S(2)}, u32[]{:S(2)}) collective-permute-start(bf16[1024,256]{1,0:T(8,128)(2,1)S(1)} %bitcast.130), channel_id=1, source_target_pairs={{0,7},{1,0},{2,1},{3,2},{4,3},{5,4},{6,5},{7,6},{8,15},{9,8},{10,9... | collective-permute-start | bytes 1572872 | tf_op jit(solution)/shard_map/ppermute | solution.py:16
  117.5 11.0 %collective-permute-done.13 = bf16[1024,256]{1,0:T(8,128)(2,1)S(1)} collective-permute-done((bf16[1024,256]{1,0:T(8,128)(2,1)S(1)}, bf16[1024,256]{1,0:T(8,128)(2,1)S(1)}, u32[]{:S(2)}, u32[]{:S(2)}) %collective-permute-start.13) | collective-permute-done | bytes 524320 | tf_op jit(solution)/shard_map/ppermute | solution.py:16
  128.5 33.7 %collective-permute-done.14 = bf16[1024,256]{1,0:T(8,128)(2,1)S(1)} collective-permute-done((bf16[1024,256]{1,0:T(8,128)(2,1)S(1)}, bf16[1024,256]{1,0:T(8,128)(2,1)S(1)}, u32[]{:S(2)}, u32[]{:S(2)}) %collective-permute-start.14) | collective-permute-done | bytes 524320 | tf_op jit(solution)/shard_map/ppermute | solution.py:16
  162.2 31.8 %collective-permute-done.15 = bf16[1024,256]{1,0:T(8,128)(2,1)S(1)} collective-permute-done((bf16[1024,256]{1,0:T(8,128)(2,1)S(1)}, bf16[1024,256]{1,0:T(8,128)(2,1)S(1)}, u32[]{:S(2)}, u32[]{:S(2)}) %collective-permute-start.15) | collective-permute-done | bytes 524320 | tf_op jit(solution)/shard_map/ppermute | solution.py:16
  195.8 2.8 gather_fusion
  212.9 7.7 %fusion = f32[1632,256]{1,0:T(8,128)} fusion(bf16[4096,256]{1,0:T(8,128)(2,1)S(1)} %bitcast.120, bf16[1632,1024]{1,0:T(8,128)(2,1)} %bitcast.140, bf16[1632,1024]{1,0:T(8,128)(2,1)} %bitcast.139, bf16[1632,1024]{1,0:T(8,128)(2,1)} %bitcast.143, bf16[1632,1024]{1,0:T(8,128)(2,1)} %bitcast.145), kind=kOutput, calls=%fused_computation.2 | convolution fusion | flops 3476029440 | bytes 17137664 | tf_op jit(solution)/shard_map/dot_general | solution.py:112
  220.6 2.8 gather_fusion.1
  234.7 7.6 %fusion.8 = f32[1632,256]{1,0:T(8,128)S(1)} fusion(bf16[4096,256]{1,0:T(8,128)(2,1)S(1)} %bitcast.119, bf16[1632,1024]{1,0:T(8,128)(2,1)} %bitcast.142, bf16[1632,1024]{1,0:T(8,128)(2,1)S(1)} %bitcast.141, bf16[1632,1024]{1,0:T(8,128)(2,1)} %bitcast.144, bf16[1632,1024]{1,0:T(8,128)(2,1)} %bitcast.146), kind=kOutput, calls=%fused_computation.10 | convolution fusion | flops 3476029440 | bytes 17137664 | tf_op jit(solution)/shard_map/dot_general | solution.py:112
  243.5 32.4 %all_to_all.10 = f32[8,32,1632]{2,1,0:T(8,128)S(1)} all-to-all(f32[8,32,1632]{2,1,0:T(8,128)S(1)} %bitcast.113), channel_id=1, replica_groups=mesh['chips'=16,'core'=2,'win'=8] {'win'}, dimensions={0} | all-to-all | bytes 3342336 | tf_op jit(solution)/shard_map/all_to_all | solution.py:126
  275.9 4.3 %copy.30 = f32[8,32,1632]{1,2,0:T(8,128)} copy(f32[8,32,1632]{2,1,0:T(8,128)S(1)} %all_to_all.10) | data formatting | bytes 3342336 | tf_op jit(solution)/shard_map/all_to_all | solution.py:126
  280.2 6.8 %copy.31 = f32[6,32,17,8,16]{1,4,3,2,0:T(8,128)} copy(f32[6,32,17,8,16]{1,4,2,0,3:T(8,128)} %bitcast.111) | data formatting | bytes 3342336 | tf_op jit(solution)/shard_map/transpose | solution.py:128
  286.9 5.7 %copy.32 = f32[6,32,2176]{2,1,0:T(8,128)} copy(f32[6,32,2176]{1,2,0:T(8,128)} %bitcast.112) | data formatting | bytes 3342336 | tf_op jit(solution)/shard_map/reshape | solution.py:129
  (224 shorter events, 42.4 us)
Async XLA Ops:
  6.5 13.7 %copy-start.10 = (bf16[321]{0:T(512)(128)(2,1)S(1)}, bf16[321]{0:T(512)(128)(2,1)}, u32[]{:S(2)}) copy-start(bf16[321]{0:T(512)(128)(2,1)} %constant.83.clone.1) | copy-start | bytes 1930
  8.8 26.4 %all-to-all-start = ((bf16[32,32,256]{2,1,0:T(8,128)(2,1)}), bf16[32,32,256]{2,1,0:T(8,128)(2,1)S(1)}, u32[]{:S(2)}, u32[]{:S(2)}) async-start(bf16[32,32,256]{2,1,0:T(8,128)(2,1)} %copy.26), calls=%async_computation | async-start | bytes 1048576 | tf_op jit(solution)/shard_map/all_to_all | solution.py:60
  18.7 177.1 %all-gather.2.cloned.1.call-start = ((), (), s32[]{:S(2)}) async-start(), calls=%async_computation.2 | async-start | bytes 4456448 | tf_op jit(solution)/shard_map/all_gather | solution.py:91
  35.9 22.1 %copy-start.12 = (s32[1,6]{1,0:T(1,128)S(1)}, s32[1,6]{1,0:T(1,128)}, u32[]{:S(2)}) copy-start(s32[1,6]{1,0:T(1,128)} %param.6) | copy-start | bytes 76
  35.9 22.3 %copy-start.11 = (s32[1,6]{1,0:T(1,128)S(1)}, s32[1,6]{1,0:T(1,128)}, u32[]{:S(2)}) copy-start(s32[1,6]{1,0:T(1,128)} %param.7) | copy-start | bytes 76
  36.8 10.3 %collective-permute-start = (bf16[16,1024]{1,0:T(8,128)(2,1)S(1)}, bf16[16,1024]{1,0:T(8,128)(2,1)S(1)}, u32[]{:S(2)}, u32[]{:S(2)}) collective-permute-start(bf16[16,1024]{1,0:T(8,128)(2,1)S(1)} %get-tuple-element.37), channel_id=1, source_target_pairs={{0,1},{1,2},{2,3},{3,4},{4,5},{5,6},{6,7},{7,0},{8,9},{9,10},{10,1... | collective-permute-start | bytes 98312 | tf_op jit(solution)/shard_map/ppermute | solution.py:16
  38.1 11.7 %collective-permute-start.1 = (bf16[16,1024]{1,0:T(8,128)(2,1)S(1)}, bf16[16,1024]{1,0:T(8,128)(2,1)S(1)}, u32[]{:S(2)}, u32[]{:S(2)}) collective-permute-start(bf16[16,1024]{1,0:T(8,128)(2,1)S(1)} %get-tuple-element.36), channel_id=1, source_target_pairs={{0,2},{1,3},{2,4},{3,5},{4,6},{5,7},{6,0},{7,1},{8,10},{9,11},{10,... | collective-permute-start | bytes 98312 | tf_op jit(solution)/shard_map/ppermute | solution.py:16
  40.8 10.5 %collective-permute-start.2 = (bf16[16,1024]{1,0:T(8,128)(2,1)S(1)}, bf16[16,1024]{1,0:T(8,128)(2,1)S(1)}, u32[]{:S(2)}, u32[]{:S(2)}) collective-permute-start(bf16[16,1024]{1,0:T(8,128)(2,1)S(1)} %get-tuple-element.35), channel_id=1, source_target_pairs={{0,3},{1,4},{2,5},{3,6},{4,7},{5,0},{6,1},{7,2},{8,11},{9,12},{10,... | collective-permute-start | bytes 98312 | tf_op jit(solution)/shard_map/ppermute | solution.py:16
  44.0 7.2 %collective-permute-start.3 = (bf16[16,1024]{1,0:T(8,128)(2,1)S(1)}, bf16[16,1024]{1,0:T(8,128)(2,1)S(1)}, u32[]{:S(2)}, u32[]{:S(2)}) collective-permute-start(bf16[16,1024]{1,0:T(8,128)(2,1)S(1)} %get-tuple-element.34), channel_id=1, source_target_pairs={{0,4},{1,5},{2,6},{3,7},{4,0},{5,1},{6,2},{7,3},{8,12},{9,13},{10,... | collective-permute-start | bytes 98312 | tf_op jit(solution)/shard_map/ppermute | solution.py:16
  44.5 6.7 %collective-permute-start.4 = (bf16[16,1024]{1,0:T(8,128)(2,1)S(1)}, bf16[16,1024]{1,0:T(8,128)(2,1)S(1)}, u32[]{:S(2)}, u32[]{:S(2)}) collective-permute-start(bf16[16,1024]{1,0:T(8,128)(2,1)S(1)} %get-tuple-element.33), channel_id=1, source_target_pairs={{0,5},{1,6},{2,7},{3,0},{4,1},{5,2},{6,3},{7,4},{8,13},{9,14},{10,... | collective-permute-start | bytes 98312 | tf_op jit(solution)/shard_map/ppermute | solution.py:16
  47.1 4.4 %collective-permute-start.5 = (bf16[16,1024]{1,0:T(8,128)(2,1)S(1)}, bf16[16,1024]{1,0:T(8,128)(2,1)S(1)}, u32[]{:S(2)}, u32[]{:S(2)}) collective-permute-start(bf16[16,1024]{1,0:T(8,128)(2,1)S(1)} %get-tuple-element.32), channel_id=1, source_target_pairs={{0,6},{1,7},{2,0},{3,1},{4,2},{5,3},{6,4},{7,5},{8,14},{9,15},{10,... | collective-permute-start | bytes 98312 | tf_op jit(solution)/shard_map/ppermute | solution.py:16
  49.8 2.8 collective-permute-start.6
  52.6 4.6 %collective-permute-start.7 = (bf16[4,16,1024]{2,1,0:T(8,128)(2,1)S(1)}, bf16[4,16,1024]{2,1,0:T(8,128)(2,1)S(1)}, u32[]{:S(2)}, u32[]{:S(2)}) collective-permute-start(bf16[4,16,1024]{2,1,0:T(8,128)(2,1)S(1)} %dynamic-slice_bitcast_fusion), channel_id=1, source_target_pairs={{0,8},{8,0},{1,9},{9,1},{2,10},{10,2},{3,11},{11,3},{4,12},{12,4},... | collective-permute-start | bytes 393224 | tf_op jit(solution)/shard_map/ppermute | solution.py:88
  58.1 27.4 %collective-permute-start.9 = (bf16[1024,256]{1,0:T(8,128)(2,1)S(1)}, bf16[1024,256]{1,0:T(8,128)(2,1)S(1)}, u32[]{:S(2)}, u32[]{:S(2)}) collective-permute-start(bf16[1024,256]{1,0:T(8,128)(2,1)S(1)} %bitcast.123), channel_id=1, source_target_pairs={{0,1},{1,2},{2,3},{3,4},{4,5},{5,6},{6,7},{7,0},{8,9},{9,10},{10,1... | collective-permute-start | bytes 1572872 | tf_op jit(solution)/shard_map/ppermute | solution.py:16
  58.3 30.7 %collective-permute-start.10 = (bf16[1024,256]{1,0:T(8,128)(2,1)S(1)}, bf16[1024,256]{1,0:T(8,128)(2,1)S(1)}, u32[]{:S(2)}, u32[]{:S(2)}) collective-permute-start(bf16[1024,256]{1,0:T(8,128)(2,1)S(1)} %bitcast.124), channel_id=1, source_target_pairs={{0,2},{1,3},{2,4},{3,5},{4,6},{5,7},{6,0},{7,1},{8,10},{9,11},{10,... | collective-permute-start | bytes 1572872 | tf_op jit(solution)/shard_map/ppermute | solution.py:16
  62.5 54.8 %collective-permute-start.11 = (bf16[1024,256]{1,0:T(8,128)(2,1)S(1)}, bf16[1024,256]{1,0:T(8,128)(2,1)S(1)}, u32[]{:S(2)}, u32[]{:S(2)}) collective-permute-start(bf16[1024,256]{1,0:T(8,128)(2,1)S(1)} %bitcast.125), channel_id=1, source_target_pairs={{0,3},{1,4},{2,5},{3,6},{4,7},{5,0},{6,1},{7,2},{8,11},{9,12},{10,... | collective-permute-start | bytes 1572872 | tf_op jit(solution)/shard_map/ppermute | solution.py:16
  64.3 53.1 %collective-permute-start.12 = (bf16[1024,256]{1,0:T(8,128)(2,1)S(1)}, bf16[1024,256]{1,0:T(8,128)(2,1)S(1)}, u32[]{:S(2)}, u32[]{:S(2)}) collective-permute-start(bf16[1024,256]{1,0:T(8,128)(2,1)S(1)} %bitcast.126), channel_id=1, source_target_pairs={{0,4},{1,5},{2,6},{3,7},{4,0},{5,1},{6,2},{7,3},{8,12},{9,13},{10,... | collective-permute-start | bytes 1572872 | tf_op jit(solution)/shard_map/ppermute | solution.py:16
  65.3 63.2 %collective-permute-start.13 = (bf16[1024,256]{1,0:T(8,128)(2,1)S(1)}, bf16[1024,256]{1,0:T(8,128)(2,1)S(1)}, u32[]{:S(2)}, u32[]{:S(2)}) collective-permute-start(bf16[1024,256]{1,0:T(8,128)(2,1)S(1)} %bitcast.127), channel_id=1, source_target_pairs={{0,5},{1,6},{2,7},{3,0},{4,1},{5,2},{6,3},{7,4},{8,13},{9,14},{10,... | collective-permute-start | bytes 1572872 | tf_op jit(solution)/shard_map/ppermute | solution.py:16
  85.5 76.7 %collective-permute-start.14 = (bf16[1024,256]{1,0:T(8,128)(2,1)S(1)}, bf16[1024,256]{1,0:T(8,128)(2,1)S(1)}, u32[]{:S(2)}, u32[]{:S(2)}) collective-permute-start(bf16[1024,256]{1,0:T(8,128)(2,1)S(1)} %bitcast.129), channel_id=1, source_target_pairs={{0,6},{1,7},{2,0},{3,1},{4,2},{5,3},{6,4},{7,5},{8,14},{9,15},{10,... | collective-permute-start | bytes 1572872 | tf_op jit(solution)/shard_map/ppermute | solution.py:16
  89.0 105.0 %collective-permute-start.15 = (bf16[1024,256]{1,0:T(8,128)(2,1)S(1)}, bf16[1024,256]{1,0:T(8,128)(2,1)S(1)}, u32[]{:S(2)}, u32[]{:S(2)}) collective-permute-start(bf16[1024,256]{1,0:T(8,128)(2,1)S(1)} %bitcast.130), channel_id=1, source_target_pairs={{0,7},{1,0},{2,1},{3,2},{4,3},{5,4},{6,5},{7,6},{8,15},{9,8},{10,9... | collective-permute-start | bytes 1572872 | tf_op jit(solution)/shard_map/ppermute | solution.py:16
  204.7 2.5 copy-start.2
  207.2 13.4 %collective-permute-start.8 = (bf16[32,4,16,1024]{3,2,1,0:T(8,128)(2,1)S(1)}, bf16[32,4,16,1024]{3,2,1,0:T(8,128)(2,1)}, u32[]{:S(2)}, u32[]{:S(2)}) collective-permute-start(bf16[32,4,16,1024]{3,2,1,0:T(8,128)(2,1)S(1)} %copy-done.2), channel_id=1, source_target_pairs={{0,8},{8,0},{1,9},{9,1},{2,10},{10,2},{3,11},{11,3},{4,12},{12,4},... | collective-permute-start | bytes 12582920 | tf_op jit(solution)/shard_map/ppermute | solution.py:92
  209.5 3.5 %copy-start = (bf16[1,4,1024,256]{3,2,1,0:T(8,128)(2,1)S(1)}, bf16[1,4,1024,256]{3,2,1,0:T(8,128)(2,1)}, u32[]{:S(2)}) copy-start(bf16[1,4,1024,256]{3,2,1,0:T(8,128)(2,1)} %get-tuple-element.10) | copy-start | bytes 6291460
  234.7 7.6 %copy-start.1 = (f32[1632,256]{1,0:T(8,128)S(1)}, f32[1632,256]{1,0:T(8,128)}, u32[]{:S(2)}) copy-start(f32[1632,256]{1,0:T(8,128)} %fusion) | copy-start | bytes 5013508
  (7 other events, 12.2 us)
Sparse Core Ops, SparseCore 0:
  58.2 137.5 all-gather.1

commit v2 on v1

--- a/solution.py
+++ b/solution.py
@@ -70,25 +70,22 @@
         pick, receivers, (((1,), (1,)), ((), ())), preferred_element_type=jnp.float32
     ).astype(receivers.dtype).reshape(n_win, group, samples)
     source_pieces = [lax.dynamic_index_in_dim(sources, me, 0, keepdims=False)]
-    receiver_pieces = [receivers]
     for distance in range(1, n_win):
         target = lax.rem(me + distance, n_win)
         source_pieces.append(
             shifted(lax.dynamic_index_in_dim(sources, target, 0, keepdims=False), "win", distance)
         )
-        receiver_pieces.append(shifted(receivers, "win", distance))
-    stack = jnp.stack(receiver_pieces)
-    panel = jnp.stack(source_pieces)
+    stack = lax.all_gather(receivers, "win", axis=0, tiled=False)
+    order = lax.rem(me - jnp.arange(n_win, dtype=jnp.int32) + n_win, n_win)
+    panel = jnp.take(jnp.stack(source_pieces), order, axis=0, mode="clip")
 
     core = lax.axis_index("core")
     half = n_win // n_core
-    share = panel.reshape(n_core, half, group, samples)
-    mine = lax.dynamic_index_in_dim(share, core, 0, keepdims=False)
-    other = lax.dynamic_index_in_dim(share, 1 - core, 0, keepdims=False)
-    sibling = lax.ppermute(other, "core", [(0, 1), (1, 0)])
-    first_is_mine = core == 0
-    pair = jnp.stack([jnp.where(first_is_mine, mine, sibling), jnp.where(first_is_mine, sibling, mine)])
-    own_half = lax.all_gather(pair, "chips", axis=0, tiled=True).reshape(n_chan, half, group, samples)
+    share = panel.reshape(1, n_core, half, group, samples)
+    share = jnp.broadcast_to(share, (n_chips, n_core, half, group, samples)).reshape(
+        n_chan, half, group, samples
+    )
+    own_half = lax.all_to_all(share, blocks_axis, 0, 0, tiled=True)
     other_half = lax.ppermute(own_half, "core", [(0, 1), (1, 0)])
 
     block = lax.axis_index("chips") * n_core + core

time: 303 us -> 270 us (0.89)
  starting transfers between devices: 68.9 us -> 35 us
  waiting for transfers between devices: 112 us -> 120 us
  blocking collectives: 32.4 us -> 25.9 us
    all_gather x1, waiting for transfers between devices: 0.11 us -> 104 us  [on_device(): stack = lax.all_gather(receivers, 'win', axis=0, tiled=False)]
    ppermute x14 -> x7, waiting for transfers between devices: 97.1 us -> 1.34 us  [shifted(): return lax.ppermute(block, axis, route)]
    ppermute x14 -> x7, starting transfers between devices: 54 us -> 14.4 us  [shifted(): return lax.ppermute(block, axis, route)]
    all_to_all x0 -> x1, starting transfers between devices: none -> 8.87 us  [on_device(): own_half = lax.all_to_all(share, blocks_axis, 0, 0, tiled=True)]
    all_to_all x1, blocking collectives: 32.4 us -> 25.9 us  [on_device(): result = lax.all_to_all(result, 'win', 0, 0, tiled=True)]
    ppermute x1 -> x0, starting transfers between devices: 3.66 us -> none  [on_device(): sibling = lax.ppermute(other, 'core', [(0, 1), (1, 0)])]
    unnamed x156 -> x145, local copies, waits for them, and re-layouts: 23.1 us -> 20 us
  transfers between devices with their start and end apart: 18 -> 11, of which waited for: 10 -> 4; matrix products, arithmetic and copies ran while one was open for 5% -> 6% of each run, Pallas kernels for 0% -> 0%
where the time goes in v2:
time: 270 us; the launch traced here: 267 us
  waiting for transfers between devices  120 us (44%)
  local copies, waits for them, and re-layouts  55.4 us (21%)
  starting transfers between devices  35 us (13%)
  blocking collectives  25.9 us (10%)
  matrix products  15.6 us (6%)
  between operations  14.7 us (5%)
    all_gather x1, waiting for transfers between devices, on_device(): stack = lax.all_gather(receivers, 'win', axis=0, tiled=False)  104 us
    all_to_all x1, blocking collectives, on_device(): result = lax.all_to_all(result, 'win', 0, 0, tiled=True)  25.9 us
    unnamed x145, local copies, waits for them, and re-layouts  20 us
    ppermute x7, starting transfers between devices, shifted(): return lax.ppermute(block, axis, route)  14.4 us
    dot_general x2, matrix products, on_device(): lax.dot_general(lagged, lax.dynamic_index_in_dim(stack, which, 0, keepdim...  14.4 us
    all_to_all x1, waiting for transfers between devices, on_device(): gathered = lax.all_to_all(blocks_first, blocks_axis, 0, 0, tiled=True)  14.2 us
    all_to_all x1, starting transfers between devices, on_device(): gathered = lax.all_to_all(blocks_first, blocks_axis, 0, 0, tiled=True)  9.94 us
    all_to_all x1, starting transfers between devices, on_device(): own_half = lax.all_to_all(share, blocks_axis, 0, 0, tiled=True)  8.87 us
  transfers between devices with their start and end apart: 11, of which 4 were waited for; matrix products, arithmetic and copies ran while one was open for 6% of the time, Pallas kernels for 0%

profile of v2, /device:TPU:33, one launch (start us, length us, event | category | flops | bytes accessed | tf_op | source)
XLA Modules:
  0.0 267.0 jit_solution(2739723271154907354)
XLA Ops:
  6.5 1.2 copy.37
  8.8 9.9 %all-to-all-start = ((bf16[32,32,256]{2,1,0:T(8,128)(2,1)}), bf16[32,32,256]{2,1,0:T(8,128)(2,1)S(1)}, u32[]{:S(2)}, u32[]{:S(2)}) async-start(bf16[32,32,256]{2,1,0:T(8,128)(2,1)} %copy.26), calls=%async_computation | async-start | bytes 1048576 | tf_op jit(solution)/shard_map/all_to_all | solution.py:60
  21.0 14.2 %all-to-all-done = bf16[32,32,256]{2,1,0:T(8,128)(2,1)S(1)} async-done(((bf16[32,32,256]{2,1,0:T(8,128)(2,1)}), bf16[32,32,256]{2,1,0:T(8,128)(2,1)S(1)}, u32[]{:S(2)}, u32[]{:S(2)}) %all-to-all-start) | async-done | bytes 524320 | tf_op jit(solution)/shard_map/all_to_all | solution.py:60
  36.7 1.4 collective-permute-start
  38.1 2.6 collective-permute-start.1
  40.7 3.2 %collective-permute-start.2 = (bf16[16,1024]{1,0:T(8,128)(2,1)S(1)}, bf16[16,1024]{1,0:T(8,128)(2,1)S(1)}, u32[]{:S(2)}, u32[]{:S(2)}) collective-permute-start(bf16[16,1024]{1,0:T(8,128)(2,1)S(1)} %get-tuple-element.33), channel_id=1, source_target_pairs={{0,3},{1,4},{2,5},{3,6},{4,7},{5,0},{6,1},{7,2},{8,11},{9,12},{10,... | collective-permute-start | bytes 98312 | tf_op jit(solution)/shard_map/ppermute | solution.py:16
  44.5 2.6 collective-permute-start.4
  47.1 2.8 %collective-permute-start.5 = (bf16[16,1024]{1,0:T(8,128)(2,1)S(1)}, bf16[16,1024]{1,0:T(8,128)(2,1)S(1)}, u32[]{:S(2)}, u32[]{:S(2)}) collective-permute-start(bf16[16,1024]{1,0:T(8,128)(2,1)S(1)} %get-tuple-element.30), channel_id=1, source_target_pairs={{0,6},{1,7},{2,0},{3,1},{4,2},{5,3},{6,4},{7,5},{8,14},{9,15},{10,... | collective-permute-start | bytes 98312 | tf_op jit(solution)/shard_map/ppermute | solution.py:16
  49.8 1.4 collective-permute-start.6
  51.5 1.1 collective-permute-done.6
  53.2 2.6 broadcast_in_dim.12
  55.7 8.9 %all-to-all-start.1 = ((bf16[32,4,16,1024]{3,2,1,0:T(8,128)(2,1)}), bf16[32,4,16,1024]{3,2,1,0:T(8,128)(2,1)}, u32[]{:S(2)}, u32[]{:S(2)}) async-start(bf16[32,4,16,1024]{3,2,1,0:T(8,128)(2,1)} %bitcast.89), calls=%async_computation.1 | async-start | bytes 8388608 | tf_op jit(solution)/shard_map/all_to_all | solution.py:88
  65.7 103.7 %all-gather.2.cloned.1.call-done = bf16[8,1024,256]{2,1,0:T(8,128)(2,1)} async-done(((bf16[1,1024,256]{2,1,0:T(8,128)(2,1)}), bf16[8,1024,256]{2,1,0:T(8,128)(2,1)}) %all-gather.2.cloned.1.call-update) | async-done | bytes 4194320 | tf_op jit(solution)/shard_map/all_gather | solution.py:78
  169.5 3.8 %constant_dynamic-slice_fusion = (bf16[1,4,1024,256]{3,2,1,0:T(8,128)(2,1)S(1)}, bf16[1,4,1024,256]{3,2,1,0:T(8,128)(2,1)}) fusion(bf16[2,4,1024,256]{3,2,1,0:T(8,128)(2,1)} %bitcast.95, s32[]{:T(128)S(6)} %select_n.41, s32[]{:T(128)S(6)} %select_n.40), kind=kLoop, calls=%fused_computation.195 | loop fusion | bytes 8388616 | tf_op jit(solution)/shard_map/jit(dynamic_index_in_dim)/dynamic_slice | solution.py:111
  173.3 2.8 %gather_fusion.1 = bf16[6,4,16,1024]{3,2,1,0:T(8,128)(2,1)S(1)} fusion(bf16[32,4,16,1024]{3,2,1,0:T(8,128)(2,1)} %all-to-all-done.1, s32[1024]{0:T(1024)S(1)} %pad_clamp_fusion), kind=kCustom, calls=%fused_computation.1 | custom fusion | bytes 1572888 | tf_op jit(solution)/shard_map/jit(_take)/gather | solution.py:102
  183.7 1.6 collective-permute-start.7
  187.8 7.0 %fusion = f32[1632,256]{1,0:T(8,128)} fusion(bf16[4096,256]{1,0:T(8,128)(2,1)S(1)} %bitcast.97, bf16[1632,1024]{1,0:T(8,128)(2,1)S(1)} %bitcast.109, bf16[1632,1024]{1,0:T(8,128)(2,1)S(1)} %bitcast.108, bf16[1632,1024]{1,0:T(8,128)(2,1)} %bitcast.112, bf16[1632,1024]{1,0:T(8,128)(2,1)} %bitcast.114), kind=kOutput, calls=%fused_computation.3 | convolution fusion | flops 3476029440 | bytes 17137664 | tf_op jit(solution)/shard_map/dot_general | solution.py:109
  194.8 2.8 %gather_fusion.2 = bf16[6,4,16,1024]{3,2,1,0:T(8,128)(2,1)S(1)} fusion(bf16[32,4,16,1024]{3,2,1,0:T(8,128)(2,1)} %collective-permute-done.7, s32[1024]{0:T(1024)S(1)} %pad_clamp_fusion), kind=kCustom, calls=%fused_computation.2 | custom fusion | bytes 1572888 | tf_op jit(solution)/shard_map/jit(_take)/gather | solution.py:102
  207.2 1.7 copy-done.3
  208.9 7.4 %fusion.8 = f32[1632,256]{1,0:T(8,128)S(1)} fusion(bf16[4096,256]{1,0:T(8,128)(2,1)S(1)} %bitcast.96, bf16[1632,1024]{1,0:T(8,128)(2,1)} %bitcast.111, bf16[1632,1024]{1,0:T(8,128)(2,1)S(1)} %bitcast.110, bf16[1632,1024]{1,0:T(8,128)(2,1)} %bitcast.113, bf16[1632,1024]{1,0:T(8,128)(2,1)} %bitcast.115), kind=kOutput, calls=%fused_computation.11 | convolution fusion | flops 3476029440 | bytes 17137664 | tf_op jit(solution)/shard_map/dot_general | solution.py:109
  217.5 25.9 %all_to_all.15 = f32[8,32,1632]{2,1,0:T(8,128)S(1)} all-to-all(f32[8,32,1632]{2,1,0:T(8,128)S(1)} %bitcast.90), channel_id=1, replica_groups=mesh['chips'=16,'core'=2,'win'=8] {'win'}, dimensions={0} | all-to-all | bytes 3342336 | tf_op jit(solution)/shard_map/all_to_all | solution.py:123
  243.4 4.3 %copy.30 = f32[8,32,1632]{1,2,0:T(8,128)} copy(f32[8,32,1632]{2,1,0:T(8,128)S(1)} %all_to_all.15) | data formatting | bytes 3342336 | tf_op jit(solution)/shard_map/all_to_all | solution.py:123
  247.6 6.8 %copy.31 = f32[6,32,17,8,16]{1,4,3,2,0:T(8,128)} copy(f32[6,32,17,8,16]{1,4,2,0,3:T(8,128)} %bitcast.87) | data formatting | bytes 3342336 | tf_op jit(solution)/shard_map/transpose | solution.py:125
  254.4 5.7 %copy.32 = f32[6,32,2176]{2,1,0:T(8,128)} copy(f32[6,32,2176]{1,2,0:T(8,128)} %bitcast.88) | data formatting | bytes 3342336 | tf_op jit(solution)/shard_map/reshape | solution.py:126
  (199 shorter events, 27.0 us)
Async XLA Ops:
  6.5 13.7 %copy-start.8 = (bf16[321]{0:T(512)(128)(2,1)S(1)}, bf16[321]{0:T(512)(128)(2,1)}, u32[]{:S(2)}) copy-start(bf16[321]{0:T(512)(128)(2,1)} %constant.77.clone.1) | copy-start | bytes 1930
  8.8 26.4 %all-to-all-start = ((bf16[32,32,256]{2,1,0:T(8,128)(2,1)}), bf16[32,32,256]{2,1,0:T(8,128)(2,1)S(1)}, u32[]{:S(2)}, u32[]{:S(2)}) async-start(bf16[32,32,256]{2,1,0:T(8,128)(2,1)} %copy.26), calls=%async_computation | async-start | bytes 1048576 | tf_op jit(solution)/shard_map/all_to_all | solution.py:60
  36.4 19.4 %copy-start.1 = (bf16[4,256,256]{1,2,0:T(8,128)(2,1)}, bf16[4,256,256]{1,2,0:T(8,128)(2,1)S(1)}, u32[]{:S(2)}) copy-start(bf16[4,256,256]{1,2,0:T(8,128)(2,1)S(1)} %fusion.18) | copy-start | bytes 1572868
  36.7 10.3 %collective-permute-start = (bf16[16,1024]{1,0:T(8,128)(2,1)S(1)}, bf16[16,1024]{1,0:T(8,128)(2,1)S(1)}, u32[]{:S(2)}, u32[]{:S(2)}) collective-permute-start(bf16[16,1024]{1,0:T(8,128)(2,1)S(1)} %get-tuple-element.35), channel_id=1, source_target_pairs={{0,1},{1,2},{2,3},{3,4},{4,5},{5,6},{6,7},{7,0},{8,9},{9,10},{10,1... | collective-permute-start | bytes 98312 | tf_op jit(solution)/shard_map/ppermute | solution.py:16
  38.1 11.7 %collective-permute-start.1 = (bf16[16,1024]{1,0:T(8,128)(2,1)S(1)}, bf16[16,1024]{1,0:T(8,128)(2,1)S(1)}, u32[]{:S(2)}, u32[]{:S(2)}) collective-permute-start(bf16[16,1024]{1,0:T(8,128)(2,1)S(1)} %get-tuple-element.34), channel_id=1, source_target_pairs={{0,2},{1,3},{2,4},{3,5},{4,6},{5,7},{6,0},{7,1},{8,10},{9,11},{10,... | collective-permute-start | bytes 98312 | tf_op jit(solution)/shard_map/ppermute | solution.py:16
  40.7 10.5 %collective-permute-start.2 = (bf16[16,1024]{1,0:T(8,128)(2,1)S(1)}, bf16[16,1024]{1,0:T(8,128)(2,1)S(1)}, u32[]{:S(2)}, u32[]{:S(2)}) collective-permute-start(bf16[16,1024]{1,0:T(8,128)(2,1)S(1)} %get-tuple-element.33), channel_id=1, source_target_pairs={{0,3},{1,4},{2,5},{3,6},{4,7},{5,0},{6,1},{7,2},{8,11},{9,12},{10,... | collective-permute-start | bytes 98312 | tf_op jit(solution)/shard_map/ppermute | solution.py:16
  44.0 7.2 %collective-permute-start.3 = (bf16[16,1024]{1,0:T(8,128)(2,1)S(1)}, bf16[16,1024]{1,0:T(8,128)(2,1)S(1)}, u32[]{:S(2)}, u32[]{:S(2)}) collective-permute-start(bf16[16,1024]{1,0:T(8,128)(2,1)S(1)} %get-tuple-element.32), channel_id=1, source_target_pairs={{0,4},{1,5},{2,6},{3,7},{4,0},{5,1},{6,2},{7,3},{8,12},{9,13},{10,... | collective-permute-start | bytes 98312 | tf_op jit(solution)/shard_map/ppermute | solution.py:16
  44.5 6.7 %collective-permute-start.4 = (bf16[16,1024]{1,0:T(8,128)(2,1)S(1)}, bf16[16,1024]{1,0:T(8,128)(2,1)S(1)}, u32[]{:S(2)}, u32[]{:S(2)}) collective-permute-start(bf16[16,1024]{1,0:T(8,128)(2,1)S(1)} %get-tuple-element.31), channel_id=1, source_target_pairs={{0,5},{1,6},{2,7},{3,0},{4,1},{5,2},{6,3},{7,4},{8,13},{9,14},{10,... | collective-permute-start | bytes 98312 | tf_op jit(solution)/shard_map/ppermute | solution.py:16
  47.1 4.4 %collective-permute-start.5 = (bf16[16,1024]{1,0:T(8,128)(2,1)S(1)}, bf16[16,1024]{1,0:T(8,128)(2,1)S(1)}, u32[]{:S(2)}, u32[]{:S(2)}) collective-permute-start(bf16[16,1024]{1,0:T(8,128)(2,1)S(1)} %get-tuple-element.30), channel_id=1, source_target_pairs={{0,6},{1,7},{2,0},{3,1},{4,2},{5,3},{6,4},{7,5},{8,14},{9,15},{10,... | collective-permute-start | bytes 98312 | tf_op jit(solution)/shard_map/ppermute | solution.py:16
  49.8 2.8 %collective-permute-start.6 = (bf16[16,1024]{1,0:T(8,128)(2,1)S(1)}, bf16[16,1024]{1,0:T(8,128)(2,1)S(1)}, u32[]{:S(2)}, u32[]{:S(2)}) collective-permute-start(bf16[16,1024]{1,0:T(8,128)(2,1)S(1)} %get-tuple-element.29), channel_id=1, source_target_pairs={{0,7},{1,0},{2,1},{3,2},{4,3},{5,4},{6,5},{7,6},{8,15},{9,8},{10,9... | collective-permute-start | bytes 98312 | tf_op jit(solution)/shard_map/ppermute | solution.py:16
  55.7 9.6 %copy-start.10 = (s32[1,6]{1,0:T(1,128)S(1)}, s32[1,6]{1,0:T(1,128)}, u32[]{:S(2)}) copy-start(s32[1,6]{1,0:T(1,128)} %param.6) | copy-start | bytes 76
  55.7 9.7 %copy-start.9 = (s32[1,6]{1,0:T(1,128)S(1)}, s32[1,6]{1,0:T(1,128)}, u32[]{:S(2)}) copy-start(s32[1,6]{1,0:T(1,128)} %param.7) | copy-start | bytes 76
  55.7 117.6 %all-to-all-start.1 = ((bf16[32,4,16,1024]{3,2,1,0:T(8,128)(2,1)}), bf16[32,4,16,1024]{3,2,1,0:T(8,128)(2,1)}, u32[]{:S(2)}, u32[]{:S(2)}) async-start(bf16[32,4,16,1024]{3,2,1,0:T(8,128)(2,1)} %bitcast.89), calls=%async_computation.1 | async-start | bytes 8388608 | tf_op jit(solution)/shard_map/all_to_all | solution.py:88
  64.6 104.9 %all-gather.2.cloned.1.call-start = ((), (), s32[]{:S(2)}) async-start(), calls=%async_computation.3 | async-start | bytes 4718592 | tf_op jit(solution)/shard_map/all_gather | solution.py:78
  178.3 1.7 copy-start.6
  181.2 1.7 copy-start.4
  183.7 11.1 %collective-permute-start.7 = (bf16[32,4,16,1024]{3,2,1,0:T(8,128)(2,1)}, bf16[32,4,16,1024]{3,2,1,0:T(8,128)(2,1)}, u32[]{:S(2)}, u32[]{:S(2)}) collective-permute-start(bf16[32,4,16,1024]{3,2,1,0:T(8,128)(2,1)} %all-to-all-done.1), channel_id=1, source_target_pairs={{0,8},{8,0},{1,9},{9,1},{2,10},{10,2},{3,11},{11,3},{4,12},{12,4},... | collective-permute-start | bytes 12582920 | tf_op jit(solution)/shard_map/ppermute | solution.py:89
  186.2 1.6 copy-start
  199.9 1.8 copy-start.7
  202.8 1.7 copy-start.5
  207.2 1.7 copy-start.3
  208.9 7.4 %copy-start.2 = (f32[1632,256]{1,0:T(8,128)S(1)}, f32[1632,256]{1,0:T(8,128)}, u32[]{:S(2)}) copy-start(f32[1632,256]{1,0:T(8,128)} %fusion) | copy-start | bytes 5013508
Sparse Core Ops, SparseCore 0:
  68.1 101.3 all-gather.1

commit v3 on v2

--- a/solution.py
+++ b/solution.py
@@ -70,14 +70,15 @@
         pick, receivers, (((1,), (1,)), ((), ())), preferred_element_type=jnp.float32
     ).astype(receivers.dtype).reshape(n_win, group, samples)
     source_pieces = [lax.dynamic_index_in_dim(sources, me, 0, keepdims=False)]
+    receiver_pieces = [receivers]
     for distance in range(1, n_win):
         target = lax.rem(me + distance, n_win)
         source_pieces.append(
             shifted(lax.dynamic_index_in_dim(sources, target, 0, keepdims=False), "win", distance)
         )
-    stack = lax.all_gather(receivers, "win", axis=0, tiled=False)
-    order = lax.rem(me - jnp.arange(n_win, dtype=jnp.int32) + n_win, n_win)
-    panel = jnp.take(jnp.stack(source_pieces), order, axis=0, mode="clip")
+        receiver_pieces.append(shifted(receivers, "win", distance))
+    stack = jnp.stack(receiver_pieces)
+    panel = jnp.stack(source_pieces)
 
     core = lax.axis_index("core")
     half = n_win // n_core

time: 270 us -> 251 us (0.930)
  waiting for transfers between devices: 120 us -> 82.5 us
  starting transfers between devices: 35 us -> 65.2 us
  between operations: 14.7 us -> 1.37 us
  blocking collectives: 25.9 us -> 31.1 us
    all_gather x1 -> x0, waiting for transfers between devices: 104 us -> none  [on_device(): stack = lax.all_gather(receivers, 'win', axis=0, tiled=False)]
    ppermute x7 -> x14, waiting for transfers between devices: 1.34 us -> 68.3 us  [shifted(): return lax.ppermute(block, axis, route)]
    ppermute x7 -> x14, starting transfers between devices: 14.4 us -> 44.4 us  [shifted(): return lax.ppermute(block, axis, route)]
    all_to_all x1, blocking collectives: 25.9 us -> 31.1 us  [on_device(): result = lax.all_to_all(result, 'win', 0, 0, tiled=True)]
    unnamed x145 -> x150, local copies, waits for them, and re-layouts: 20 us -> 20.3 us
  transfers between devices with their start and end apart: 11 -> 17, of which waited for: 4 -> 6; matrix products, arithmetic and copies ran while one was open for 6% -> 5% of each run, Pallas kernels for 0% -> 0%
where the time goes in v3:
time: 251 us; the launch traced here: 249 us
  waiting for transfers between devices  82.5 us (33%)
  starting transfers between devices  65.2 us (26%)
  local copies, waits for them, and re-layouts  53 us (21%)
  blocking collectives  31.1 us (12%)
  matrix products  15.8 us (6%)
    ppermute x14, waiting for transfers between devices, shifted(): return lax.ppermute(block, axis, route)  68.3 us
    ppermute x14, starting transfers between devices, shifted(): return lax.ppermute(block, axis, route)  44.4 us
    all_to_all x1, blocking collectives, on_device(): result = lax.all_to_all(result, 'win', 0, 0, tiled=True)  31.1 us
    unnamed x150, local copies, waits for them, and re-layouts  20.3 us
    dot_general x2, matrix products, on_device(): lax.dot_general(lagged, lax.dynamic_index_in_dim(stack, which, 0, keepdim...  14.6 us
    all_to_all x1, waiting for transfers between devices, on_device(): gathered = lax.all_to_all(blocks_first, blocks_axis, 0, 0, tiled=True)  14.2 us
    all_to_all x1, starting transfers between devices, on_device(): gathered = lax.all_to_all(blocks_first, blocks_axis, 0, 0, tiled=True)  9.94 us
    all_to_all x1, starting transfers between devices, on_device(): own_half = lax.all_to_all(share, blocks_axis, 0, 0, tiled=True)  8.86 us
  transfers between devices with their start and end apart: 17, of which 6 were waited for; matrix products, arithmetic and copies ran while one was open for 5% of the time, Pallas kernels for 0%

profile of v3, /device:TPU:33, one launch (start us, length us, event | category | flops | bytes accessed | tf_op | source)
XLA Modules:
  0.0 249.3 jit_solution(8025167490732799968)
XLA Ops:
  2.3 9.9 %all-to-all-start = ((bf16[32,32,256]{2,1,0:T(8,128)(2,1)}), bf16[32,32,256]{2,1,0:T(8,128)(2,1)S(1)}, u32[]{:S(2)}, u32[]{:S(2)}) async-start(bf16[32,32,256]{2,1,0:T(8,128)(2,1)} %copy.26), calls=%async_computation | async-start | bytes 1048576 | tf_op jit(solution)/shard_map/all_to_all | solution.py:60
  14.5 14.2 %all-to-all-done = bf16[32,32,256]{2,1,0:T(8,128)(2,1)S(1)} async-done(((bf16[32,32,256]{2,1,0:T(8,128)(2,1)}), bf16[32,32,256]{2,1,0:T(8,128)(2,1)S(1)}, u32[]{:S(2)}, u32[]{:S(2)}) %all-to-all-start) | async-done | bytes 524320 | tf_op jit(solution)/shard_map/all_to_all | solution.py:60
  31.6 2.6 %collective-permute-start.1 = (bf16[16,1024]{1,0:T(8,128)(2,1)S(1)}, bf16[16,1024]{1,0:T(8,128)(2,1)S(1)}, u32[]{:S(2)}, u32[]{:S(2)}) collective-permute-start(bf16[16,1024]{1,0:T(8,128)(2,1)S(1)} %get-tuple-element.34), channel_id=1, source_target_pairs={{0,2},{1,3},{2,4},{3,5},{4,6},{5,7},{6,0},{7,1},{8,10},{9,11},{10,... | collective-permute-start | bytes 98312 | tf_op jit(solution)/shard_map/ppermute | solution.py:16
  34.2 3.2 %collective-permute-start.2 = (bf16[16,1024]{1,0:T(8,128)(2,1)S(1)}, bf16[16,1024]{1,0:T(8,128)(2,1)S(1)}, u32[]{:S(2)}, u32[]{:S(2)}) collective-permute-start(bf16[16,1024]{1,0:T(8,128)(2,1)S(1)} %get-tuple-element.33), channel_id=1, source_target_pairs={{0,3},{1,4},{2,5},{3,6},{4,7},{5,0},{6,1},{7,2},{8,11},{9,12},{10,... | collective-permute-start | bytes 98312 | tf_op jit(solution)/shard_map/ppermute | solution.py:16
  38.0 2.6 %collective-permute-start.4 = (bf16[16,1024]{1,0:T(8,128)(2,1)S(1)}, bf16[16,1024]{1,0:T(8,128)(2,1)S(1)}, u32[]{:S(2)}, u32[]{:S(2)}) collective-permute-start(bf16[16,1024]{1,0:T(8,128)(2,1)S(1)} %get-tuple-element.31), channel_id=1, source_target_pairs={{0,5},{1,6},{2,7},{3,0},{4,1},{5,2},{6,3},{7,4},{8,13},{9,14},{10,... | collective-permute-start | bytes 98312 | tf_op jit(solution)/shard_map/ppermute | solution.py:16
  40.5 2.8 %collective-permute-start.5 = (bf16[16,1024]{1,0:T(8,128)(2,1)S(1)}, bf16[16,1024]{1,0:T(8,128)(2,1)S(1)}, u32[]{:S(2)}, u32[]{:S(2)}) collective-permute-start(bf16[16,1024]{1,0:T(8,128)(2,1)S(1)} %get-tuple-element.30), channel_id=1, source_target_pairs={{0,6},{1,7},{2,0},{3,1},{4,2},{5,3},{6,4},{7,5},{8,14},{9,15},{10,... | collective-permute-start | bytes 98312 | tf_op jit(solution)/shard_map/ppermute | solution.py:16
  46.1 2.6 %broadcast_in_dim.10 = bf16[16,2,4,16,1024]{4,3,2,1,0:T(8,128)(2,1)} broadcast(bf16[2,4,16,1024]{3,2,1,0:T(8,128)(2,1)S(1)} %bitcast.126), dimensions={1,2,3,4} | broadcast | bytes 4456448 | tf_op jit(solution)/shard_map/broadcast_in_dim | solution.py:86
  48.6 8.9 %all-to-all-start.1 = ((bf16[32,4,16,1024]{3,2,1,0:T(8,128)(2,1)}), bf16[32,4,16,1024]{3,2,1,0:T(8,128)(2,1)}, u32[]{:S(2)}, u32[]{:S(2)}) async-start(bf16[32,4,16,1024]{3,2,1,0:T(8,128)(2,1)} %bitcast.101), calls=%async_computation.1 | async-start | bytes 8388608 | tf_op jit(solution)/shard_map/all_to_all | solution.py:89
  57.8 3.9 %collective-permute-start.9 = (bf16[1024,256]{1,0:T(8,128)(2,1)S(1)}, bf16[1024,256]{1,0:T(8,128)(2,1)S(1)}, u32[]{:S(2)}, u32[]{:S(2)}) collective-permute-start(bf16[1024,256]{1,0:T(8,128)(2,1)S(1)} %bitcast.113), channel_id=1, source_target_pairs={{0,2},{1,3},{2,4},{3,5},{4,6},{5,7},{6,0},{7,1},{8,10},{9,11},{10,... | collective-permute-start | bytes 1572872 | tf_op jit(solution)/shard_map/ppermute | solution.py:16
  62.0 1.8 collective-permute-start.10
  64.8 3.6 %collective-permute-start.12 = (bf16[1024,256]{1,0:T(8,128)(2,1)S(1)}, bf16[1024,256]{1,0:T(8,128)(2,1)S(1)}, u32[]{:S(2)}, u32[]{:S(2)}) collective-permute-start(bf16[1024,256]{1,0:T(8,128)(2,1)S(1)} %bitcast.116), channel_id=1, source_target_pairs={{0,5},{1,6},{2,7},{3,0},{4,1},{5,2},{6,3},{7,4},{8,13},{9,14},{10,... | collective-permute-start | bytes 1572872 | tf_op jit(solution)/shard_map/ppermute | solution.py:16
  68.4 28.7 %collective-permute-done.8 = bf16[1024,256]{1,0:T(8,128)(2,1)S(1)} collective-permute-done((bf16[1024,256]{1,0:T(8,128)(2,1)S(1)}, bf16[1024,256]{1,0:T(8,128)(2,1)S(1)}, u32[]{:S(2)}, u32[]{:S(2)}) %collective-permute-start.8) | collective-permute-done | bytes 524320 | tf_op jit(solution)/shard_map/ppermute | solution.py:16
  97.1 19.5 %collective-permute-start.14 = (bf16[1024,256]{1,0:T(8,128)(2,1)S(1)}, bf16[1024,256]{1,0:T(8,128)(2,1)S(1)}, u32[]{:S(2)}, u32[]{:S(2)}) collective-permute-start(bf16[1024,256]{1,0:T(8,128)(2,1)S(1)} %bitcast.119), channel_id=1, source_target_pairs={{0,7},{1,0},{2,1},{3,2},{4,3},{5,4},{6,5},{7,6},{8,15},{9,8},{10,9... | collective-permute-start | bytes 1572872 | tf_op jit(solution)/shard_map/ppermute | solution.py:16
  116.8 17.3 %collective-permute-done.13 = bf16[1024,256]{1,0:T(8,128)(2,1)S(1)} collective-permute-done((bf16[1024,256]{1,0:T(8,128)(2,1)S(1)}, bf16[1024,256]{1,0:T(8,128)(2,1)S(1)}, u32[]{:S(2)}, u32[]{:S(2)}) %collective-permute-start.13) | collective-permute-done | bytes 524320 | tf_op jit(solution)/shard_map/ppermute | solution.py:16
  134.2 20.9 %collective-permute-done.14 = bf16[1024,256]{1,0:T(8,128)(2,1)S(1)} collective-permute-done((bf16[1024,256]{1,0:T(8,128)(2,1)S(1)}, bf16[1024,256]{1,0:T(8,128)(2,1)S(1)}, u32[]{:S(2)}, u32[]{:S(2)}) %collective-permute-start.14) | collective-permute-done | bytes 524320 | tf_op jit(solution)/shard_map/ppermute | solution.py:16
  156.7 2.8 %gather_fusion = bf16[6,4,16,1024]{3,2,1,0:T(8,128)(2,1)S(1)} fusion(bf16[32,4,16,1024]{3,2,1,0:T(8,128)(2,1)} %all-to-all-done.1, s32[1024]{0:T(1024)S(1)} %pad_clamp_fusion), kind=kCustom, calls=%fused_computation | custom fusion | bytes 1572888 | tf_op jit(solution)/shard_map/jit(_take)/gather | solution.py:103
  167.2 1.9 collective-permute-start.7
  171.7 7.0 %fusion = f32[1632,256]{1,0:T(8,128)} fusion(bf16[4096,256]{1,0:T(8,128)(2,1)S(1)} %bitcast.109, bf16[1632,1024]{1,0:T(8,128)(2,1)S(1)} %bitcast.128, bf16[1632,1024]{1,0:T(8,128)(2,1)S(1)} %bitcast.127, bf16[1632,1024]{1,0:T(8,128)(2,1)} %bitcast.131, bf16[1632,1024]{1,0:T(8,128)(2,1)} %bitcast.133), kind=kOutput, calls=%fused_computation.2 | convolution fusion | flops 3476029440 | bytes 17137664 | tf_op jit(solution)/shard_map/dot_general | solution.py:110
  178.7 2.8 %gather_fusion.1 = bf16[6,4,16,1024]{3,2,1,0:T(8,128)(2,1)S(1)} fusion(bf16[32,4,16,1024]{3,2,1,0:T(8,128)(2,1)} %collective-permute-done.7, s32[1024]{0:T(1024)S(1)} %pad_clamp_fusion), kind=kCustom, calls=%fused_computation.1 | custom fusion | bytes 1572888 | tf_op jit(solution)/shard_map/jit(_take)/gather | solution.py:103
  192.7 7.6 %fusion.8 = f32[1632,256]{1,0:T(8,128)S(1)} fusion(bf16[4096,256]{1,0:T(8,128)(2,1)S(1)} %bitcast.108, bf16[1632,1024]{1,0:T(8,128)(2,1)} %bitcast.130, bf16[1632,1024]{1,0:T(8,128)(2,1)S(1)} %bitcast.129, bf16[1632,1024]{1,0:T(8,128)(2,1)} %bitcast.132, bf16[1632,1024]{1,0:T(8,128)(2,1)} %bitcast.134), kind=kOutput, calls=%fused_computation.10 | convolution fusion | flops 3476029440 | bytes 17137664 | tf_op jit(solution)/shard_map/dot_general | solution.py:110
  201.5 31.1 %all_to_all.15 = f32[8,32,1632]{2,1,0:T(8,128)S(1)} all-to-all(f32[8,32,1632]{2,1,0:T(8,128)S(1)} %bitcast.102), channel_id=1, replica_groups=mesh['chips'=16,'core'=2,'win'=8] {'win'}, dimensions={0} | all-to-all | bytes 3342336 | tf_op jit(solution)/shard_map/all_to_all | solution.py:124
  232.6 4.3 %copy.30 = f32[8,32,1632]{1,2,0:T(8,128)} copy(f32[8,32,1632]{2,1,0:T(8,128)S(1)} %all_to_all.15) | data formatting | bytes 3342336 | tf_op jit(solution)/shard_map/all_to_all | solution.py:124
  236.9 6.8 %copy.31 = f32[6,32,17,8,16]{1,4,3,2,0:T(8,128)} copy(f32[6,32,17,8,16]{1,4,2,0,3:T(8,128)} %bitcast.99) | data formatting | bytes 3342336 | tf_op jit(solution)/shard_map/transpose | solution.py:126
  243.6 5.7 %copy.32 = f32[6,32,2176]{2,1,0:T(8,128)} copy(f32[6,32,2176]{1,2,0:T(8,128)} %bitcast.100) | data formatting | bytes 3342336 | tf_op jit(solution)/shard_map/reshape | solution.py:127
  (213 shorter events, 35.6 us)
Async XLA Ops:
  0.0 13.7 %copy-start.7 = (bf16[321]{0:T(512)(128)(2,1)S(1)}, bf16[321]{0:T(512)(128)(2,1)}, u32[]{:S(2)}) copy-start(bf16[321]{0:T(512)(128)(2,1)} %constant.74.clone.1) | copy-start | bytes 1930
  2.3 26.4 %all-to-all-start = ((bf16[32,32,256]{2,1,0:T(8,128)(2,1)}), bf16[32,32,256]{2,1,0:T(8,128)(2,1)S(1)}, u32[]{:S(2)}, u32[]{:S(2)}) async-start(bf16[32,32,256]{2,1,0:T(8,128)(2,1)} %copy.26), calls=%async_computation | async-start | bytes 1048576 | tf_op jit(solution)/shard_map/all_to_all | solution.py:60
  30.2 10.3 %collective-permute-start = (bf16[16,1024]{1,0:T(8,128)(2,1)S(1)}, bf16[16,1024]{1,0:T(8,128)(2,1)S(1)}, u32[]{:S(2)}, u32[]{:S(2)}) collective-permute-start(bf16[16,1024]{1,0:T(8,128)(2,1)S(1)} %get-tuple-element.35), channel_id=1, source_target_pairs={{0,1},{1,2},{2,3},{3,4},{4,5},{5,6},{6,7},{7,0},{8,9},{9,10},{10,1... | collective-permute-start | bytes 98312 | tf_op jit(solution)/shard_map/ppermute | solution.py:16
  31.6 11.7 %collective-permute-start.1 = (bf16[16,1024]{1,0:T(8,128)(2,1)S(1)}, bf16[16,1024]{1,0:T(8,128)(2,1)S(1)}, u32[]{:S(2)}, u32[]{:S(2)}) collective-permute-start(bf16[16,1024]{1,0:T(8,128)(2,1)S(1)} %get-tuple-element.34), channel_id=1, source_target_pairs={{0,2},{1,3},{2,4},{3,5},{4,6},{5,7},{6,0},{7,1},{8,10},{9,11},{10,... | collective-permute-start | bytes 98312 | tf_op jit(solution)/shard_map/ppermute | solution.py:16
  34.2 10.5 %collective-permute-start.2 = (bf16[16,1024]{1,0:T(8,128)(2,1)S(1)}, bf16[16,1024]{1,0:T(8,128)(2,1)S(1)}, u32[]{:S(2)}, u32[]{:S(2)}) collective-permute-start(bf16[16,1024]{1,0:T(8,128)(2,1)S(1)} %get-tuple-element.33), channel_id=1, source_target_pairs={{0,3},{1,4},{2,5},{3,6},{4,7},{5,0},{6,1},{7,2},{8,11},{9,12},{10,... | collective-permute-start | bytes 98312 | tf_op jit(solution)/shard_map/ppermute | solution.py:16
  37.4 7.2 %collective-permute-start.3 = (bf16[16,1024]{1,0:T(8,128)(2,1)S(1)}, bf16[16,1024]{1,0:T(8,128)(2,1)S(1)}, u32[]{:S(2)}, u32[]{:S(2)}) collective-permute-start(bf16[16,1024]{1,0:T(8,128)(2,1)S(1)} %get-tuple-element.32), channel_id=1, source_target_pairs={{0,4},{1,5},{2,6},{3,7},{4,0},{5,1},{6,2},{7,3},{8,12},{9,13},{10,... | collective-permute-start | bytes 98312 | tf_op jit(solution)/shard_map/ppermute | solution.py:16
  38.0 6.7 %collective-permute-start.4 = (bf16[16,1024]{1,0:T(8,128)(2,1)S(1)}, bf16[16,1024]{1,0:T(8,128)(2,1)S(1)}, u32[]{:S(2)}, u32[]{:S(2)}) collective-permute-start(bf16[16,1024]{1,0:T(8,128)(2,1)S(1)} %get-tuple-element.31), channel_id=1, source_target_pairs={{0,5},{1,6},{2,7},{3,0},{4,1},{5,2},{6,3},{7,4},{8,13},{9,14},{10,... | collective-permute-start | bytes 98312 | tf_op jit(solution)/shard_map/ppermute | solution.py:16
  40.5 4.4 %collective-permute-start.5 = (bf16[16,1024]{1,0:T(8,128)(2,1)S(1)}, bf16[16,1024]{1,0:T(8,128)(2,1)S(1)}, u32[]{:S(2)}, u32[]{:S(2)}) collective-permute-start(bf16[16,1024]{1,0:T(8,128)(2,1)S(1)} %get-tuple-element.30), channel_id=1, source_target_pairs={{0,6},{1,7},{2,0},{3,1},{4,2},{5,3},{6,4},{7,5},{8,14},{9,15},{10,... | collective-permute-start | bytes 98312 | tf_op jit(solution)/shard_map/ppermute | solution.py:16
  43.3 2.8 %collective-permute-start.6 = (bf16[16,1024]{1,0:T(8,128)(2,1)S(1)}, bf16[16,1024]{1,0:T(8,128)(2,1)S(1)}, u32[]{:S(2)}, u32[]{:S(2)}) collective-permute-start(bf16[16,1024]{1,0:T(8,128)(2,1)S(1)} %get-tuple-element.29), channel_id=1, source_target_pairs={{0,7},{1,0},{2,1},{3,2},{4,3},{5,4},{6,5},{7,6},{8,15},{9,8},{10,9... | collective-permute-start | bytes 98312 | tf_op jit(solution)/shard_map/ppermute | solution.py:16
  48.6 8.9 %copy-start.9 = (s32[1,6]{1,0:T(1,128)S(1)}, s32[1,6]{1,0:T(1,128)}, u32[]{:S(2)}) copy-start(s32[1,6]{1,0:T(1,128)} %param.6) | copy-start | bytes 76
  48.6 9.1 %copy-start.8 = (s32[1,6]{1,0:T(1,128)S(1)}, s32[1,6]{1,0:T(1,128)}, u32[]{:S(2)}) copy-start(s32[1,6]{1,0:T(1,128)} %param.7) | copy-start | bytes 76
  48.6 108.1 %all-to-all-start.1 = ((bf16[32,4,16,1024]{3,2,1,0:T(8,128)(2,1)}), bf16[32,4,16,1024]{3,2,1,0:T(8,128)(2,1)}, u32[]{:S(2)}, u32[]{:S(2)}) async-start(bf16[32,4,16,1024]{3,2,1,0:T(8,128)(2,1)} %bitcast.101), calls=%async_computation.1 | async-start | bytes 8388608 | tf_op jit(solution)/shard_map/all_to_all | solution.py:89
  57.5 39.5 %collective-permute-start.8 = (bf16[1024,256]{1,0:T(8,128)(2,1)S(1)}, bf16[1024,256]{1,0:T(8,128)(2,1)S(1)}, u32[]{:S(2)}, u32[]{:S(2)}) collective-permute-start(bf16[1024,256]{1,0:T(8,128)(2,1)S(1)} %bitcast.112), channel_id=1, source_target_pairs={{0,1},{1,2},{2,3},{3,4},{4,5},{5,6},{6,7},{7,0},{8,9},{9,10},{10,1... | collective-permute-start | bytes 1572872 | tf_op jit(solution)/shard_map/ppermute | solution.py:16
  57.8 39.3 %collective-permute-start.9 = (bf16[1024,256]{1,0:T(8,128)(2,1)S(1)}, bf16[1024,256]{1,0:T(8,128)(2,1)S(1)}, u32[]{:S(2)}, u32[]{:S(2)}) collective-permute-start(bf16[1024,256]{1,0:T(8,128)(2,1)S(1)} %bitcast.113), channel_id=1, source_target_pairs={{0,2},{1,3},{2,4},{3,5},{4,6},{5,7},{6,0},{7,1},{8,10},{9,11},{10,... | collective-permute-start | bytes 1572872 | tf_op jit(solution)/shard_map/ppermute | solution.py:16
  62.0 54.7 %collective-permute-start.10 = (bf16[1024,256]{1,0:T(8,128)(2,1)S(1)}, bf16[1024,256]{1,0:T(8,128)(2,1)S(1)}, u32[]{:S(2)}, u32[]{:S(2)}) collective-permute-start(bf16[1024,256]{1,0:T(8,128)(2,1)S(1)} %bitcast.114), channel_id=1, source_target_pairs={{0,3},{1,4},{2,5},{3,6},{4,7},{5,0},{6,1},{7,2},{8,11},{9,12},{10,... | collective-permute-start | bytes 1572872 | tf_op jit(solution)/shard_map/ppermute | solution.py:16
  63.7 53.0 %collective-permute-start.11 = (bf16[1024,256]{1,0:T(8,128)(2,1)S(1)}, bf16[1024,256]{1,0:T(8,128)(2,1)S(1)}, u32[]{:S(2)}, u32[]{:S(2)}) collective-permute-start(bf16[1024,256]{1,0:T(8,128)(2,1)S(1)} %bitcast.115), channel_id=1, source_target_pairs={{0,4},{1,5},{2,6},{3,7},{4,0},{5,1},{6,2},{7,3},{8,12},{9,13},{10,... | collective-permute-start | bytes 1572872 | tf_op jit(solution)/shard_map/ppermute | solution.py:16
  64.8 52.0 %collective-permute-start.12 = (bf16[1024,256]{1,0:T(8,128)(2,1)S(1)}, bf16[1024,256]{1,0:T(8,128)(2,1)S(1)}, u32[]{:S(2)}, u32[]{:S(2)}) collective-permute-start(bf16[1024,256]{1,0:T(8,128)(2,1)S(1)} %bitcast.116), channel_id=1, source_target_pairs={{0,5},{1,6},{2,7},{3,0},{4,1},{5,2},{6,3},{7,4},{8,13},{9,14},{10,... | collective-permute-start | bytes 1572872 | tf_op jit(solution)/shard_map/ppermute | solution.py:16
  97.1 37.1 %collective-permute-start.13 = (bf16[1024,256]{1,0:T(8,128)(2,1)S(1)}, bf16[1024,256]{1,0:T(8,128)(2,1)S(1)}, u32[]{:S(2)}, u32[]{:S(2)}) collective-permute-start(bf16[1024,256]{1,0:T(8,128)(2,1)S(1)} %bitcast.118), channel_id=1, source_target_pairs={{0,6},{1,7},{2,0},{3,1},{4,2},{5,3},{6,4},{7,5},{8,14},{9,15},{10,... | collective-permute-start | bytes 1572872 | tf_op jit(solution)/shard_map/ppermute | solution.py:16
  97.1 58.0 %collective-permute-start.14 = (bf16[1024,256]{1,0:T(8,128)(2,1)S(1)}, bf16[1024,256]{1,0:T(8,128)(2,1)S(1)}, u32[]{:S(2)}, u32[]{:S(2)}) collective-permute-start(bf16[1024,256]{1,0:T(8,128)(2,1)S(1)} %bitcast.119), channel_id=1, source_target_pairs={{0,7},{1,0},{2,1},{3,2},{4,3},{5,4},{6,5},{7,6},{8,15},{9,8},{10,9... | collective-permute-start | bytes 1572872 | tf_op jit(solution)/shard_map/ppermute | solution.py:16
  161.8 1.7 copy-start.5
  167.2 11.5 %collective-permute-start.7 = (bf16[32,4,16,1024]{3,2,1,0:T(8,128)(2,1)}, bf16[32,4,16,1024]{3,2,1,0:T(8,128)(2,1)}, u32[]{:S(2)}, u32[]{:S(2)}) collective-permute-start(bf16[32,4,16,1024]{3,2,1,0:T(8,128)(2,1)} %all-to-all-done.1), channel_id=1, source_target_pairs={{0,8},{8,0},{1,9},{9,1},{2,10},{10,2},{3,11},{11,3},{4,12},{12,4},... | collective-permute-start | bytes 12582920 | tf_op jit(solution)/shard_map/ppermute | solution.py:90
  183.7 1.8 copy-start.6
  186.7 1.7 copy-start.4
  192.7 7.6 %copy-start.1 = (f32[1632,256]{1,0:T(8,128)S(1)}, f32[1632,256]{1,0:T(8,128)}, u32[]{:S(2)}) copy-start(f32[1632,256]{1,0:T(8,128)} %fusion) | copy-start | bytes 5013508
  (3 other events, 5.0 us)

commit v4 on v3

--- a/solution.py
+++ b/solution.py
@@ -76,9 +76,20 @@
         source_pieces.append(
             shifted(lax.dynamic_index_in_dim(sources, target, 0, keepdims=False), "win", distance)
         )
-        receiver_pieces.append(shifted(receivers, "win", distance))
-    stack = jnp.stack(receiver_pieces)
-    panel = jnp.stack(source_pieces)
+
+    ring = n_win // 2
+    x_part = me // ring
+    y_part = me % ring
+    for distance in range(1, ring):
+        route = [(i, (i // ring) * ring + (i % ring + distance) % ring) for i in range(n_win)]
+        receiver_pieces.append(lax.ppermute(receivers, "win", route))
+    near = jnp.stack(receiver_pieces)
+    far = lax.ppermute(near, "win", [(i, (i + ring) % n_win) for i in range(n_win)])
+    stack = jnp.concatenate([near, far])
+    position = jnp.arange(n_win, dtype=jnp.int32)
+    window_of = ((x_part + position // ring) % 2) * ring + (y_part - position % ring + ring) % ring
+    piece_of = lax.rem(me - window_of + n_win, n_win)
+    panel = jnp.take(jnp.stack(source_pieces), piece_of, axis=0, mode="clip")
 
     core = lax.axis_index("core")
     half = n_win // n_core

time: 251 us -> 253 us (level)
  starting transfers between devices: 65.2 us -> 40.7 us
  waiting for transfers between devices: 82.5 us -> 106 us
    ppermute x0 -> x4, waiting for transfers between devices: none -> 90.8 us  [the longest x1 67.8 us: on_device(): lax.ppermute(near, 'win', [(i, (i + ring) % n_win) for i in range(n_win)])]
    ppermute x14 -> x7, waiting for transfers between devices: 68.3 us -> 1.34 us  [shifted(): return lax.ppermute(block, axis, route)]
    ppermute x14 -> x7, starting transfers between devices: 44.4 us -> 14.4 us  [shifted(): return lax.ppermute(block, axis, route)]
    ppermute x0 -> x4, starting transfers between devices: none -> 6.54 us  [the longest x3 4.09 us: on_device(): receiver_pieces.append(lax.ppermute(receivers, 'win', route))]
    unnamed x150 -> x153, local copies, waits for them, and re-layouts: 20.3 us -> 22 us
  transfers between devices with their start and end apart: 17 -> 14, of which waited for: 6 -> 6; matrix products, arithmetic and copies ran while one was open for 5% -> 6% of each run, Pallas kernels for 0% -> 0%
where the time goes in v4:
time: 253 us; the launch traced here: 250 us
  waiting for transfers between devices  106 us (42%)
  local copies, waits for them, and re-layouts  55.4 us (22%)
  starting transfers between devices  40.7 us (16%)
  blocking collectives  28.8 us (11%)
  matrix products  15.6 us (6%)
    ppermute x1, waiting for transfers between devices, on_device(): lax.ppermute(near, 'win', [(i, (i + ring) % n_win) for i in range(n_win)])  67.8 us
    all_to_all x1, blocking collectives, on_device(): result = lax.all_to_all(result, 'win', 0, 0, tiled=True)  28.8 us
    ppermute x3, waiting for transfers between devices, on_device(): receiver_pieces.append(lax.ppermute(receivers, 'win', route))  23 us
    unnamed x153, local copies, waits for them, and re-layouts  22 us
    ppermute x7, starting transfers between devices, shifted(): return lax.ppermute(block, axis, route)  14.4 us
    dot_general x2, matrix products, on_device(): lax.dot_general(lagged, lax.dynamic_index_in_dim(stack, which, 0, keepdim...  14.4 us
    all_to_all x1, waiting for transfers between devices, on_device(): gathered = lax.all_to_all(blocks_first, blocks_axis, 0, 0, tiled=True)  14.1 us
    all_to_all x1, starting transfers between devices, on_device(): gathered = lax.all_to_all(blocks_first, blocks_axis, 0, 0, tiled=True)  9.94 us
  transfers between devices with their start and end apart: 14, of which 6 were waited for; matrix products, arithmetic and copies ran while one was open for 6% of the time, Pallas kernels for 0%

profile of v4, /device:TPU:33, one launch (start us, length us, event | category | flops | bytes accessed | tf_op | source)
XLA Modules:
  0.0 250.3 jit_solution(2843497325233947052)
XLA Ops:
  2.3 9.9 %all-to-all-start = ((bf16[32,32,256]{2,1,0:T(8,128)(2,1)}), bf16[32,32,256]{2,1,0:T(8,128)(2,1)S(1)}, u32[]{:S(2)}, u32[]{:S(2)}) async-start(bf16[32,32,256]{2,1,0:T(8,128)(2,1)} %copy.26), calls=%async_computation | async-start | bytes 1048576 | tf_op jit(solution)/shard_map/all_to_all | solution.py:60
  14.5 14.1 %all-to-all-done = bf16[32,32,256]{2,1,0:T(8,128)(2,1)S(1)} async-done(((bf16[32,32,256]{2,1,0:T(8,128)(2,1)}), bf16[32,32,256]{2,1,0:T(8,128)(2,1)S(1)}, u32[]{:S(2)}, u32[]{:S(2)}) %all-to-all-start) | async-done | bytes 524320 | tf_op jit(solution)/shard_map/all_to_all | solution.py:60
  31.6 2.6 %collective-permute-start.1 = (bf16[16,1024]{1,0:T(8,128)(2,1)S(1)}, bf16[16,1024]{1,0:T(8,128)(2,1)S(1)}, u32[]{:S(2)}, u32[]{:S(2)}) collective-permute-start(bf16[16,1024]{1,0:T(8,128)(2,1)S(1)} %get-tuple-element.34), channel_id=1, source_target_pairs={{0,2},{1,3},{2,4},{3,5},{4,6},{5,7},{6,0},{7,1},{8,10},{9,11},{10,... | collective-permute-start | bytes 98312 | tf_op jit(solution)/shard_map/ppermute | solution.py:16
  34.2 3.2 %collective-permute-start.2 = (bf16[16,1024]{1,0:T(8,128)(2,1)S(1)}, bf16[16,1024]{1,0:T(8,128)(2,1)S(1)}, u32[]{:S(2)}, u32[]{:S(2)}) collective-permute-start(bf16[16,1024]{1,0:T(8,128)(2,1)S(1)} %get-tuple-element.33), channel_id=1, source_target_pairs={{0,3},{1,4},{2,5},{3,6},{4,7},{5,0},{6,1},{7,2},{8,11},{9,12},{10,... | collective-permute-start | bytes 98312 | tf_op jit(solution)/shard_map/ppermute | solution.py:16
  38.0 2.6 %collective-permute-start.4 = (bf16[16,1024]{1,0:T(8,128)(2,1)S(1)}, bf16[16,1024]{1,0:T(8,128)(2,1)S(1)}, u32[]{:S(2)}, u32[]{:S(2)}) collective-permute-start(bf16[16,1024]{1,0:T(8,128)(2,1)S(1)} %get-tuple-element.31), channel_id=1, source_target_pairs={{0,5},{1,6},{2,7},{3,0},{4,1},{5,2},{6,3},{7,4},{8,13},{9,14},{10,... | collective-permute-start | bytes 98312 | tf_op jit(solution)/shard_map/ppermute | solution.py:16
  40.5 2.8 %collective-permute-start.5 = (bf16[16,1024]{1,0:T(8,128)(2,1)S(1)}, bf16[16,1024]{1,0:T(8,128)(2,1)S(1)}, u32[]{:S(2)}, u32[]{:S(2)}) collective-permute-start(bf16[16,1024]{1,0:T(8,128)(2,1)S(1)} %get-tuple-element.30), channel_id=1, source_target_pairs={{0,6},{1,7},{2,0},{3,1},{4,2},{5,3},{6,4},{7,5},{8,14},{9,15},{10,... | collective-permute-start | bytes 98312 | tf_op jit(solution)/shard_map/ppermute | solution.py:16
  46.6 2.6 %broadcast_in_dim.12 = bf16[16,2,4,16,1024]{4,3,2,1,0:T(8,128)(2,1)} broadcast(bf16[2,4,16,1024]{3,2,1,0:T(8,128)(2,1)S(1)} %bitcast.115), dimensions={1,2,3,4} | broadcast | bytes 4456448 | tf_op jit(solution)/shard_map/broadcast_in_dim | solution.py:97
  49.2 8.7 %all-to-all-start.1 = ((bf16[32,4,16,1024]{3,2,1,0:T(8,128)(2,1)}), bf16[32,4,16,1024]{3,2,1,0:T(8,128)(2,1)}, u32[]{:S(2)}, u32[]{:S(2)}) async-start(bf16[32,4,16,1024]{3,2,1,0:T(8,128)(2,1)} %bitcast.95), calls=%async_computation.1 | async-start | bytes 8388608 | tf_op jit(solution)/shard_map/all_to_all | solution.py:100
  58.1 3.9 %collective-permute-start.9 = (bf16[1024,256]{1,0:T(8,128)(2,1)S(1)}, bf16[1024,256]{1,0:T(8,128)(2,1)S(1)}, u32[]{:S(2)}, u32[]{:S(2)}) collective-permute-start(bf16[1024,256]{1,0:T(8,128)(2,1)S(1)} %bitcast.104), channel_id=1, source_target_pairs={{0,2},{1,3},{2,0},{3,1},{4,6},{5,7},{6,4},{7,5},{8,10},{9,11},{10,... | collective-permute-start | bytes 1572872 | tf_op jit(solution)/shard_map/ppermute | solution.py:85
  62.0 10.7 %collective-permute-done.8 = bf16[1024,256]{1,0:T(8,128)(2,1)S(1)} collective-permute-done((bf16[1024,256]{1,0:T(8,128)(2,1)S(1)}, bf16[1024,256]{1,0:T(8,128)(2,1)S(1)}, u32[]{:S(2)}, u32[]{:S(2)}) %collective-permute-start.8) | collective-permute-done | bytes 524320 | tf_op jit(solution)/shard_map/ppermute | solution.py:85
  72.7 12.3 %collective-permute-done.9 = bf16[1024,256]{1,0:T(8,128)(2,1)S(1)} collective-permute-done((bf16[1024,256]{1,0:T(8,128)(2,1)S(1)}, bf16[1024,256]{1,0:T(8,128)(2,1)S(1)}, u32[]{:S(2)}, u32[]{:S(2)}) %collective-permute-start.9) | collective-permute-done | bytes 524320 | tf_op jit(solution)/shard_map/ppermute | solution.py:85
  85.8 1.6 pad_maximum_fusion
  87.4 2.4 collective-permute-start.11
  91.5 67.8 %collective-permute-done.11 = bf16[4,1024,256]{2,1,0:T(8,128)(2,1)S(1)} collective-permute-done((bf16[4,1024,256]{2,1,0:T(8,128)(2,1)}, bf16[4,1024,256]{2,1,0:T(8,128)(2,1)S(1)}, u32[]{:S(2)}, u32[]{:S(2)}) %collective-permute-start.11) | collective-permute-done | bytes 2097184 | tf_op jit(solution)/shard_map/ppermute | solution.py:87
  159.5 1.6 constant_dynamic-slice_fusion
  161.1 2.8 %gather_fusion.1 = bf16[6,4,16,1024]{3,2,1,0:T(8,128)(2,1)S(1)} fusion(bf16[32,4,16,1024]{3,2,1,0:T(8,128)(2,1)} %all-to-all-done.1, s32[1024]{0:T(1024)S(1)} %pad_clamp_fusion), kind=kCustom, calls=%fused_computation.1 | custom fusion | bytes 1572888 | tf_op jit(solution)/shard_map/jit(_take)/gather | solution.py:114
  175.1 7.0 %fusion = f32[1632,256]{1,0:T(8,128)} fusion(bf16[4096,256]{1,0:T(8,128)(2,1)S(1)} %bitcast.109, bf16[1632,1024]{1,0:T(8,128)(2,1)S(1)} %bitcast.122, bf16[1632,1024]{1,0:T(8,128)(2,1)S(1)} %bitcast.121, bf16[1632,1024]{1,0:T(8,128)(2,1)} %bitcast.125, bf16[1632,1024]{1,0:T(8,128)(2,1)} %bitcast.127), kind=kOutput, calls=%fused_computation.3 | convolution fusion | flops 3476029440 | bytes 17137664 | tf_op jit(solution)/shard_map/dot_general | solution.py:121
  182.1 2.8 %gather_fusion.2 = bf16[6,4,16,1024]{3,2,1,0:T(8,128)(2,1)S(1)} fusion(bf16[32,4,16,1024]{3,2,1,0:T(8,128)(2,1)} %collective-permute-done.7, s32[1024]{0:T(1024)S(1)} %pad_clamp_fusion), kind=kCustom, calls=%fused_computation.2 | custom fusion | bytes 1572888 | tf_op jit(solution)/shard_map/jit(_take)/gather | solution.py:114
  194.5 1.7 copy-done.5
  196.1 7.4 %fusion.8 = f32[1632,256]{1,0:T(8,128)S(1)} fusion(bf16[4096,256]{1,0:T(8,128)(2,1)S(1)} %bitcast.108, bf16[1632,1024]{1,0:T(8,128)(2,1)} %bitcast.124, bf16[1632,1024]{1,0:T(8,128)(2,1)S(1)} %bitcast.123, bf16[1632,1024]{1,0:T(8,128)(2,1)} %bitcast.126, bf16[1632,1024]{1,0:T(8,128)(2,1)} %bitcast.128), kind=kOutput, calls=%fused_computation.11 | convolution fusion | flops 3476029440 | bytes 17137664 | tf_op jit(solution)/shard_map/dot_general | solution.py:121
  204.7 28.8 %all_to_all.15 = f32[8,32,1632]{2,1,0:T(8,128)S(1)} all-to-all(f32[8,32,1632]{2,1,0:T(8,128)S(1)} %bitcast.96), channel_id=1, replica_groups=mesh['chips'=16,'core'=2,'win'=8] {'win'}, dimensions={0} | all-to-all | bytes 3342336 | tf_op jit(solution)/shard_map/all_to_all | solution.py:135
  233.5 4.3 %copy.30 = f32[8,32,1632]{1,2,0:T(8,128)} copy(f32[8,32,1632]{2,1,0:T(8,128)S(1)} %all_to_all.15) | data formatting | bytes 3342336 | tf_op jit(solution)/shard_map/all_to_all | solution.py:135
  237.8 6.8 %copy.31 = f32[6,32,17,8,16]{1,4,3,2,0:T(8,128)} copy(f32[6,32,17,8,16]{1,4,2,0,3:T(8,128)} %bitcast.93) | data formatting | bytes 3342336 | tf_op jit(solution)/shard_map/transpose | solution.py:137
  244.6 5.7 %copy.32 = f32[6,32,2176]{2,1,0:T(8,128)} copy(f32[6,32,2176]{1,2,0:T(8,128)} %bitcast.94) | data formatting | bytes 3342336 | tf_op jit(solution)/shard_map/reshape | solution.py:138
  (214 shorter events, 34.8 us)
Async XLA Ops:
  0.0 13.7 %copy-start.10 = (bf16[321]{0:T(512)(128)(2,1)S(1)}, bf16[321]{0:T(512)(128)(2,1)}, u32[]{:S(2)}) copy-start(bf16[321]{0:T(512)(128)(2,1)} %constant.130.clone.1) | copy-start | bytes 1930
  2.3 26.4 %all-to-all-start = ((bf16[32,32,256]{2,1,0:T(8,128)(2,1)}), bf16[32,32,256]{2,1,0:T(8,128)(2,1)S(1)}, u32[]{:S(2)}, u32[]{:S(2)}) async-start(bf16[32,32,256]{2,1,0:T(8,128)(2,1)} %copy.26), calls=%async_computation | async-start | bytes 1048576 | tf_op jit(solution)/shard_map/all_to_all | solution.py:60
  30.2 10.3 %collective-permute-start = (bf16[16,1024]{1,0:T(8,128)(2,1)S(1)}, bf16[16,1024]{1,0:T(8,128)(2,1)S(1)}, u32[]{:S(2)}, u32[]{:S(2)}) collective-permute-start(bf16[16,1024]{1,0:T(8,128)(2,1)S(1)} %get-tuple-element.35), channel_id=1, source_target_pairs={{0,1},{1,2},{2,3},{3,4},{4,5},{5,6},{6,7},{7,0},{8,9},{9,10},{10,1... | collective-permute-start | bytes 98312 | tf_op jit(solution)/shard_map/ppermute | solution.py:16
  31.6 11.7 %collective-permute-start.1 = (bf16[16,1024]{1,0:T(8,128)(2,1)S(1)}, bf16[16,1024]{1,0:T(8,128)(2,1)S(1)}, u32[]{:S(2)}, u32[]{:S(2)}) collective-permute-start(bf16[16,1024]{1,0:T(8,128)(2,1)S(1)} %get-tuple-element.34), channel_id=1, source_target_pairs={{0,2},{1,3},{2,4},{3,5},{4,6},{5,7},{6,0},{7,1},{8,10},{9,11},{10,... | collective-permute-start | bytes 98312 | tf_op jit(solution)/shard_map/ppermute | solution.py:16
  34.2 10.5 %collective-permute-start.2 = (bf16[16,1024]{1,0:T(8,128)(2,1)S(1)}, bf16[16,1024]{1,0:T(8,128)(2,1)S(1)}, u32[]{:S(2)}, u32[]{:S(2)}) collective-permute-start(bf16[16,1024]{1,0:T(8,128)(2,1)S(1)} %get-tuple-element.33), channel_id=1, source_target_pairs={{0,3},{1,4},{2,5},{3,6},{4,7},{5,0},{6,1},{7,2},{8,11},{9,12},{10,... | collective-permute-start | bytes 98312 | tf_op jit(solution)/shard_map/ppermute | solution.py:16
  37.4 7.2 %collective-permute-start.3 = (bf16[16,1024]{1,0:T(8,128)(2,1)S(1)}, bf16[16,1024]{1,0:T(8,128)(2,1)S(1)}, u32[]{:S(2)}, u32[]{:S(2)}) collective-permute-start(bf16[16,1024]{1,0:T(8,128)(2,1)S(1)} %get-tuple-element.32), channel_id=1, source_target_pairs={{0,4},{1,5},{2,6},{3,7},{4,0},{5,1},{6,2},{7,3},{8,12},{9,13},{10,... | collective-permute-start | bytes 98312 | tf_op jit(solution)/shard_map/ppermute | solution.py:16
  38.0 6.7 %collective-permute-start.4 = (bf16[16,1024]{1,0:T(8,128)(2,1)S(1)}, bf16[16,1024]{1,0:T(8,128)(2,1)S(1)}, u32[]{:S(2)}, u32[]{:S(2)}) collective-permute-start(bf16[16,1024]{1,0:T(8,128)(2,1)S(1)} %get-tuple-element.31), channel_id=1, source_target_pairs={{0,5},{1,6},{2,7},{3,0},{4,1},{5,2},{6,3},{7,4},{8,13},{9,14},{10,... | collective-permute-start | bytes 98312 | tf_op jit(solution)/shard_map/ppermute | solution.py:16
  40.5 4.4 %collective-permute-start.5 = (bf16[16,1024]{1,0:T(8,128)(2,1)S(1)}, bf16[16,1024]{1,0:T(8,128)(2,1)S(1)}, u32[]{:S(2)}, u32[]{:S(2)}) collective-permute-start(bf16[16,1024]{1,0:T(8,128)(2,1)S(1)} %get-tuple-element.30), channel_id=1, source_target_pairs={{0,6},{1,7},{2,0},{3,1},{4,2},{5,3},{6,4},{7,5},{8,14},{9,15},{10,... | collective-permute-start | bytes 98312 | tf_op jit(solution)/shard_map/ppermute | solution.py:16
  43.3 2.8 %collective-permute-start.6 = (bf16[16,1024]{1,0:T(8,128)(2,1)S(1)}, bf16[16,1024]{1,0:T(8,128)(2,1)S(1)}, u32[]{:S(2)}, u32[]{:S(2)}) collective-permute-start(bf16[16,1024]{1,0:T(8,128)(2,1)S(1)} %get-tuple-element.29), channel_id=1, source_target_pairs={{0,7},{1,0},{2,1},{3,2},{4,3},{5,4},{6,5},{7,6},{8,15},{9,8},{10,9... | collective-permute-start | bytes 98312 | tf_op jit(solution)/shard_map/ppermute | solution.py:16
  49.2 111.9 %all-to-all-start.1 = ((bf16[32,4,16,1024]{3,2,1,0:T(8,128)(2,1)}), bf16[32,4,16,1024]{3,2,1,0:T(8,128)(2,1)}, u32[]{:S(2)}, u32[]{:S(2)}) async-start(bf16[32,4,16,1024]{3,2,1,0:T(8,128)(2,1)} %bitcast.95), calls=%async_computation.1 | async-start | bytes 8388608 | tf_op jit(solution)/shard_map/all_to_all | solution.py:100
  57.9 32.0 %copy-start.12 = (s32[1,6]{1,0:T(1,128)S(1)}, s32[1,6]{1,0:T(1,128)}, u32[]{:S(2)}) copy-start(s32[1,6]{1,0:T(1,128)} %param.6) | copy-start | bytes 76
  57.9 32.0 %copy-start.11 = (s32[1,6]{1,0:T(1,128)S(1)}, s32[1,6]{1,0:T(1,128)}, u32[]{:S(2)}) copy-start(s32[1,6]{1,0:T(1,128)} %param.7) | copy-start | bytes 76
  57.9 14.8 %collective-permute-start.8 = (bf16[1024,256]{1,0:T(8,128)(2,1)S(1)}, bf16[1024,256]{1,0:T(8,128)(2,1)S(1)}, u32[]{:S(2)}, u32[]{:S(2)}) collective-permute-start(bf16[1024,256]{1,0:T(8,128)(2,1)S(1)} %bitcast.103), channel_id=1, source_target_pairs={{0,1},{1,2},{2,3},{3,0},{4,5},{5,6},{6,7},{7,4},{8,9},{9,10},{10,1... | collective-permute-start | bytes 1572872 | tf_op jit(solution)/shard_map/ppermute | solution.py:85
  58.1 26.9 %collective-permute-start.9 = (bf16[1024,256]{1,0:T(8,128)(2,1)S(1)}, bf16[1024,256]{1,0:T(8,128)(2,1)S(1)}, u32[]{:S(2)}, u32[]{:S(2)}) collective-permute-start(bf16[1024,256]{1,0:T(8,128)(2,1)S(1)} %bitcast.104), channel_id=1, source_target_pairs={{0,2},{1,3},{2,0},{3,1},{4,6},{5,7},{6,4},{7,5},{8,10},{9,11},{10,... | collective-permute-start | bytes 1572872 | tf_op jit(solution)/shard_map/ppermute | solution.py:85
  62.0 23.0 %collective-permute-start.10 = (bf16[1024,256]{1,0:T(8,128)(2,1)S(1)}, bf16[1024,256]{1,0:T(8,128)(2,1)S(1)}, u32[]{:S(2)}, u32[]{:S(2)}) collective-permute-start(bf16[1024,256]{1,0:T(8,128)(2,1)S(1)} %bitcast.105), channel_id=1, source_target_pairs={{0,3},{1,0},{2,1},{3,2},{4,7},{5,4},{6,5},{7,6},{8,11},{9,8},{10,9... | collective-permute-start | bytes 1572872 | tf_op jit(solution)/shard_map/ppermute | solution.py:85
  85.0 2.4 copy-start.2
  87.4 71.9 %collective-permute-start.11 = (bf16[4,1024,256]{2,1,0:T(8,128)(2,1)}, bf16[4,1024,256]{2,1,0:T(8,128)(2,1)S(1)}, u32[]{:S(2)}, u32[]{:S(2)}) collective-permute-start(bf16[4,1024,256]{2,1,0:T(8,128)(2,1)} %pad_maximum_fusion), channel_id=1, source_target_pairs={{0,4},{1,5},{2,6},{3,7},{4,0},{5,1},{6,2},{7,3},{8,12},{9,13},{10,... | collective-permute-start | bytes 6291464 | tf_op jit(solution)/shard_map/ppermute | solution.py:87
  166.1 1.7 copy-start.8
  169.0 1.7 copy-start.6
  171.5 10.6 %collective-permute-start.7 = (bf16[32,4,16,1024]{3,2,1,0:T(8,128)(2,1)}, bf16[32,4,16,1024]{3,2,1,0:T(8,128)(2,1)}, u32[]{:S(2)}, u32[]{:S(2)}) collective-permute-start(bf16[32,4,16,1024]{3,2,1,0:T(8,128)(2,1)} %all-to-all-done.1), channel_id=1, source_target_pairs={{0,8},{8,0},{1,9},{9,1},{2,10},{10,2},{3,11},{11,3},{4,12},{12,4},... | collective-permute-start | bytes 12582920 | tf_op jit(solution)/shard_map/ppermute | solution.py:101
  187.1 1.8 copy-start.9
  190.1 1.7 copy-start.7
  194.4 1.7 copy-start.5
  196.1 7.4 %copy-start.4 = (f32[1632,256]{1,0:T(8,128)S(1)}, f32[1632,256]{1,0:T(8,128)}, u32[]{:S(2)}) copy-start(f32[1632,256]{1,0:T(8,128)} %fusion) | copy-start | bytes 5013508
  (3 other events, 3.6 us)

commit v5 on v4

--- a/solution.py
+++ b/solution.py
@@ -83,9 +83,9 @@
     for distance in range(1, ring):
         route = [(i, (i // ring) * ring + (i % ring + distance) % ring) for i in range(n_win)]
         receiver_pieces.append(lax.ppermute(receivers, "win", route))
-    near = jnp.stack(receiver_pieces)
-    far = lax.ppermute(near, "win", [(i, (i + ring) % n_win) for i in range(n_win)])
-    stack = jnp.concatenate([near, far])
+    flip = [(i, (i + ring) % n_win) for i in range(n_win)]
+    far_pieces = [lax.ppermute(one, "win", flip) for one in receiver_pieces]
+    stack = jnp.stack(receiver_pieces + far_pieces)
     position = jnp.arange(n_win, dtype=jnp.int32)
     window_of = ((x_part + position // ring) % 2) * ring + (y_part - position % ring + ring) % ring
     piece_of = lax.rem(me - window_of + n_win, n_win)

time: 253 us -> 247 us (0.976)
  waiting for transfers between devices: 106 us -> 95.7 us
  starting transfers between devices: 40.7 us -> 47.1 us
    ppermute x1 -> x4, waiting for transfers between devices: 67.8 us -> 60.8 us  [on_device(): far_pieces = [lax.ppermute(one, 'win', flip) for one in receiver_pieces]]
    ppermute x1 -> x4, starting transfers between devices: 2.45 us -> 8.35 us  [on_device(): far_pieces = [lax.ppermute(one, 'win', flip) for one in receiver_pieces]]
    ppermute x3, waiting for transfers between devices: 23 us -> 17.1 us  [on_device(): receiver_pieces.append(lax.ppermute(receivers, 'win', route))]
    unnamed x153 -> x150, local copies, waits for them, and re-layouts: 22 us -> 20.3 us
  transfers between devices with their start and end apart: 14 -> 17, of which waited for: 6 -> 10; matrix products, arithmetic and copies ran while one was open for 6% -> 5% of each run, Pallas kernels for 0% -> 0%
where the time goes in v5:
time: 247 us; the launch traced here: 244 us
  waiting for transfers between devices  95.7 us (39%)
  local copies, waits for them, and re-layouts  54.5 us (22%)
  starting transfers between devices  47.1 us (19%)
  blocking collectives  29.5 us (12%)
  matrix products  15.7 us (6%)
    ppermute x4, waiting for transfers between devices, on_device(): far_pieces = [lax.ppermute(one, 'win', flip) for one in receiver_pieces]  60.8 us
    all_to_all x1, blocking collectives, on_device(): result = lax.all_to_all(result, 'win', 0, 0, tiled=True)  29.5 us
    unnamed x150, local copies, waits for them, and re-layouts  20.3 us
    ppermute x3, waiting for transfers between devices, on_device(): receiver_pieces.append(lax.ppermute(receivers, 'win', route))  17.1 us
    dot_general x2, matrix products, on_device(): lax.dot_general(lagged, lax.dynamic_index_in_dim(stack, which, 0, keepdim...  14.5 us
    ppermute x7, starting transfers between devices, shifted(): return lax.ppermute(block, axis, route)  14.4 us
    all_to_all x1, waiting for transfers between devices, on_device(): gathered = lax.all_to_all(blocks_first, blocks_axis, 0, 0, tiled=True)  14.1 us
    all_to_all x1, starting transfers between devices, on_device(): gathered = lax.all_to_all(blocks_first, blocks_axis, 0, 0, tiled=True)  9.94 us
  transfers between devices with their start and end apart: 17, of which 10 were waited for; matrix products, arithmetic and copies ran while one was open for 5% of the time, Pallas kernels for 0%

profile of v5, /device:TPU:33, one launch (start us, length us, event | category | flops | bytes accessed | tf_op | source)
XLA Modules:
  0.0 244.0 jit_solution(7453111661207608141)
XLA Ops:
  2.3 9.9 %all-to-all-start = ((bf16[32,32,256]{2,1,0:T(8,128)(2,1)}), bf16[32,32,256]{2,1,0:T(8,128)(2,1)S(1)}, u32[]{:S(2)}, u32[]{:S(2)}) async-start(bf16[32,32,256]{2,1,0:T(8,128)(2,1)} %copy.26), calls=%async_computation | async-start | bytes 1048576 | tf_op jit(solution)/shard_map/all_to_all | solution.py:60
  14.5 14.1 %all-to-all-done = bf16[32,32,256]{2,1,0:T(8,128)(2,1)S(1)} async-done(((bf16[32,32,256]{2,1,0:T(8,128)(2,1)}), bf16[32,32,256]{2,1,0:T(8,128)(2,1)S(1)}, u32[]{:S(2)}, u32[]{:S(2)}) %all-to-all-start) | async-done | bytes 524320 | tf_op jit(solution)/shard_map/all_to_all | solution.py:60
  31.6 2.6 %collective-permute-start.1 = (bf16[16,1024]{1,0:T(8,128)(2,1)S(1)}, bf16[16,1024]{1,0:T(8,128)(2,1)S(1)}, u32[]{:S(2)}, u32[]{:S(2)}) collective-permute-start(bf16[16,1024]{1,0:T(8,128)(2,1)S(1)} %get-tuple-element.34), channel_id=1, source_target_pairs={{0,2},{1,3},{2,4},{3,5},{4,6},{5,7},{6,0},{7,1},{8,10},{9,11},{10,... | collective-permute-start | bytes 98312 | tf_op jit(solution)/shard_map/ppermute | solution.py:16
  34.2 3.2 %collective-permute-start.2 = (bf16[16,1024]{1,0:T(8,128)(2,1)S(1)}, bf16[16,1024]{1,0:T(8,128)(2,1)S(1)}, u32[]{:S(2)}, u32[]{:S(2)}) collective-permute-start(bf16[16,1024]{1,0:T(8,128)(2,1)S(1)} %get-tuple-element.33), channel_id=1, source_target_pairs={{0,3},{1,4},{2,5},{3,6},{4,7},{5,0},{6,1},{7,2},{8,11},{9,12},{10,... | collective-permute-start | bytes 98312 | tf_op jit(solution)/shard_map/ppermute | solution.py:16
  40.5 2.8 %collective-permute-start.5 = (bf16[16,1024]{1,0:T(8,128)(2,1)S(1)}, bf16[16,1024]{1,0:T(8,128)(2,1)S(1)}, u32[]{:S(2)}, u32[]{:S(2)}) collective-permute-start(bf16[16,1024]{1,0:T(8,128)(2,1)S(1)} %get-tuple-element.30), channel_id=1, source_target_pairs={{0,6},{1,7},{2,0},{3,1},{4,2},{5,3},{6,4},{7,5},{8,14},{9,15},{10,... | collective-permute-start | bytes 98312 | tf_op jit(solution)/shard_map/ppermute | solution.py:16
  46.6 2.6 %broadcast_in_dim.12 = bf16[16,2,4,16,1024]{4,3,2,1,0:T(8,128)(2,1)} broadcast(bf16[2,4,16,1024]{3,2,1,0:T(8,128)(2,1)S(1)} %bitcast.120), dimensions={1,2,3,4} | broadcast | bytes 4456448 | tf_op jit(solution)/shard_map/broadcast_in_dim | solution.py:97
  49.2 8.9 %all-to-all-start.1 = ((bf16[32,4,16,1024]{3,2,1,0:T(8,128)(2,1)}), bf16[32,4,16,1024]{3,2,1,0:T(8,128)(2,1)}, u32[]{:S(2)}, u32[]{:S(2)}) async-start(bf16[32,4,16,1024]{3,2,1,0:T(8,128)(2,1)} %bitcast.103), calls=%async_computation.1 | async-start | bytes 8388608 | tf_op jit(solution)/shard_map/all_to_all | solution.py:100
  58.3 3.9 %collective-permute-start.9 = (bf16[1024,256]{1,0:T(8,128)(2,1)S(1)}, bf16[1024,256]{1,0:T(8,128)(2,1)S(1)}, u32[]{:S(2)}, u32[]{:S(2)}) collective-permute-start(bf16[1024,256]{1,0:T(8,128)(2,1)S(1)} %bitcast.115), channel_id=1, source_target_pairs={{0,2},{1,3},{2,0},{3,1},{4,6},{5,7},{6,4},{7,5},{8,10},{9,11},{10,... | collective-permute-start | bytes 1572872 | tf_op jit(solution)/shard_map/ppermute | solution.py:85
  62.6 2.7 %collective-permute-start.11 = (bf16[1024,256]{1,0:T(8,128)(2,1)S(1)}, bf16[1024,256]{1,0:T(8,128)(2,1)S(1)}, u32[]{:S(2)}, u32[]{:S(2)}) collective-permute-start(bf16[1024,256]{1,0:T(8,128)(2,1)S(1)} %bitcast.117), channel_id=1, source_target_pairs={{0,4},{1,5},{2,6},{3,7},{4,0},{5,1},{6,2},{7,3},{8,12},{9,13},{10,... | collective-permute-start | bytes 1572872 | tf_op jit(solution)/shard_map/ppermute | solution.py:87
  65.4 7.5 %collective-permute-done.8 = bf16[1024,256]{1,0:T(8,128)(2,1)S(1)} collective-permute-done((bf16[1024,256]{1,0:T(8,128)(2,1)S(1)}, bf16[1024,256]{1,0:T(8,128)(2,1)S(1)}, u32[]{:S(2)}, u32[]{:S(2)}) %collective-permute-start.8) | collective-permute-done | bytes 524320 | tf_op jit(solution)/shard_map/ppermute | solution.py:85
  72.9 2.6 %collective-permute-start.12 = (bf16[1024,256]{1,0:T(8,128)(2,1)S(1)}, bf16[1024,256]{1,0:T(8,128)(2,1)S(1)}, u32[]{:S(2)}, u32[]{:S(2)}) collective-permute-start(bf16[1024,256]{1,0:T(8,128)(2,1)S(1)} %collective-permute-done.8), channel_id=1, source_target_pairs={{0,4},{1,5},{2,6},{3,7},{4,0},{5,1},{6,2},{7,3},{8,12},{9,13},{10,... | collective-permute-start | bytes 1572872 | tf_op jit(solution)/shard_map/ppermute | solution.py:87
  75.5 9.6 %collective-permute-done.9 = bf16[1024,256]{1,0:T(8,128)(2,1)S(1)} collective-permute-done((bf16[1024,256]{1,0:T(8,128)(2,1)S(1)}, bf16[1024,256]{1,0:T(8,128)(2,1)S(1)}, u32[]{:S(2)}, u32[]{:S(2)}) %collective-permute-start.9) | collective-permute-done | bytes 524320 | tf_op jit(solution)/shard_map/ppermute | solution.py:85
  88.3 5.0 %collective-permute-done.11 = bf16[1024,256]{1,0:T(8,128)(2,1)S(1)} collective-permute-done((bf16[1024,256]{1,0:T(8,128)(2,1)S(1)}, bf16[1024,256]{1,0:T(8,128)(2,1)S(1)}, u32[]{:S(2)}, u32[]{:S(2)}) %collective-permute-start.11) | collective-permute-done | bytes 524320 | tf_op jit(solution)/shard_map/ppermute | solution.py:87
  93.3 16.6 %collective-permute-done.12 = bf16[1024,256]{1,0:T(8,128)(2,1)S(1)} collective-permute-done((bf16[1024,256]{1,0:T(8,128)(2,1)S(1)}, bf16[1024,256]{1,0:T(8,128)(2,1)S(1)}, u32[]{:S(2)}, u32[]{:S(2)}) %collective-permute-start.12) | collective-permute-done | bytes 524320 | tf_op jit(solution)/shard_map/ppermute | solution.py:87
  110.0 26.3 %collective-permute-done.13 = bf16[1024,256]{1,0:T(8,128)(2,1)S(1)} collective-permute-done((bf16[1024,256]{1,0:T(8,128)(2,1)S(1)}, bf16[1024,256]{1,0:T(8,128)(2,1)S(1)}, u32[]{:S(2)}, u32[]{:S(2)}) %collective-permute-start.13) | collective-permute-done | bytes 524320 | tf_op jit(solution)/shard_map/ppermute | solution.py:87
  136.3 12.9 %collective-permute-done.14 = bf16[1024,256]{1,0:T(8,128)(2,1)S(1)} collective-permute-done((bf16[1024,256]{1,0:T(8,128)(2,1)S(1)}, bf16[1024,256]{1,0:T(8,128)(2,1)S(1)}, u32[]{:S(2)}, u32[]{:S(2)}) %collective-permute-start.14) | collective-permute-done | bytes 524320 | tf_op jit(solution)/shard_map/ppermute | solution.py:87
  153.1 2.8 %gather_fusion.1 = bf16[6,4,16,1024]{3,2,1,0:T(8,128)(2,1)S(1)} fusion(bf16[32,4,16,1024]{3,2,1,0:T(8,128)(2,1)} %all-to-all-done.1, s32[1024]{0:T(1024)S(1)} %pad_clamp_fusion), kind=kCustom, calls=%fused_computation.1 | custom fusion | bytes 1572888 | tf_op jit(solution)/shard_map/jit(_take)/gather | solution.py:114
  167.3 7.0 %fusion = f32[1632,256]{1,0:T(8,128)} fusion(bf16[4096,256]{1,0:T(8,128)(2,1)S(1)} %bitcast.111, bf16[1632,1024]{1,0:T(8,128)(2,1)S(1)} %bitcast.127, bf16[1632,1024]{1,0:T(8,128)(2,1)S(1)} %bitcast.126, bf16[1632,1024]{1,0:T(8,128)(2,1)} %bitcast.130, bf16[1632,1024]{1,0:T(8,128)(2,1)} %bitcast.132), kind=kOutput, calls=%fused_computation.3 | convolution fusion | flops 3476029440 | bytes 17137664 | tf_op jit(solution)/shard_map/dot_general | solution.py:121
  174.4 2.8 %gather_fusion.2 = bf16[6,4,16,1024]{3,2,1,0:T(8,128)(2,1)S(1)} fusion(bf16[32,4,16,1024]{3,2,1,0:T(8,128)(2,1)} %collective-permute-done.7, s32[1024]{0:T(1024)S(1)} %pad_clamp_fusion), kind=kCustom, calls=%fused_computation.2 | custom fusion | bytes 1572888 | tf_op jit(solution)/shard_map/jit(_take)/gather | solution.py:114
  188.4 7.5 %multiply_bitcast_fusion = f32[256,1632]{0,1:T(8,128)} fusion(f32[1632,256]{1,0:T(8,128)S(1)} %copy-done.9, f32[1632]{0:T(1024)S(1)} %mul.74, bf16[4096,256]{1,0:T(8,128)(2,1)S(1)} %bitcast.110, bf16[1632,1024]{1,0:T(8,128)(2,1)} %bitcast.129, bf16[1632,1024]{1,0:T(8,128)(2,1)S(1)} %bitcast.128, bf16[1632,1024]{1,0:T(8,128)(2,1)} %bitcast.131, ...), kind=kOutput, calls=%fused_computation.19 | convolution fusion | flops 3476865024 | bytes 18815360 | tf_op jit(solution)/shard_map/dot_general | solution.py:121
  197.7 29.5 %all_to_all.15 = f32[8,32,1632]{2,1,0:T(8,128)S(1)} all-to-all(f32[8,32,1632]{2,1,0:T(8,128)S(1)} %bitcast.104), channel_id=1, replica_groups=mesh['chips'=16,'core'=2,'win'=8] {'win'}, dimensions={0} | all-to-all | bytes 3342336 | tf_op jit(solution)/shard_map/all_to_all | solution.py:135
  227.2 4.3 %copy.30 = f32[8,32,1632]{1,2,0:T(8,128)} copy(f32[8,32,1632]{2,1,0:T(8,128)S(1)} %all_to_all.15) | data formatting | bytes 3342336 | tf_op jit(solution)/shard_map/all_to_all | solution.py:135
  231.5 6.8 %copy.31 = f32[6,32,17,8,16]{1,4,3,2,0:T(8,128)} copy(f32[6,32,17,8,16]{1,4,2,0,3:T(8,128)} %bitcast.101) | data formatting | bytes 3342336 | tf_op jit(solution)/shard_map/transpose | solution.py:137
  238.3 5.7 %copy.32 = f32[6,32,2176]{2,1,0:T(8,128)} copy(f32[6,32,2176]{1,2,0:T(8,128)} %bitcast.102) | data formatting | bytes 3342336 | tf_op jit(solution)/shard_map/reshape | solution.py:138
  (215 shorter events, 45.0 us)
Async XLA Ops:
  0.0 13.7 %copy-start.6 = (bf16[321]{0:T(512)(128)(2,1)S(1)}, bf16[321]{0:T(512)(128)(2,1)}, u32[]{:S(2)}) copy-start(bf16[321]{0:T(512)(128)(2,1)} %constant.130.clone.1) | copy-start | bytes 1930
  2.3 26.4 %all-to-all-start = ((bf16[32,32,256]{2,1,0:T(8,128)(2,1)}), bf16[32,32,256]{2,1,0:T(8,128)(2,1)S(1)}, u32[]{:S(2)}, u32[]{:S(2)}) async-start(bf16[32,32,256]{2,1,0:T(8,128)(2,1)} %copy.26), calls=%async_computation | async-start | bytes 1048576 | tf_op jit(solution)/shard_map/all_to_all | solution.py:60
  30.2 10.3 %collective-permute-start = (bf16[16,1024]{1,0:T(8,128)(2,1)S(1)}, bf16[16,1024]{1,0:T(8,128)(2,1)S(1)}, u32[]{:S(2)}, u32[]{:S(2)}) collective-permute-start(bf16[16,1024]{1,0:T(8,128)(2,1)S(1)} %get-tuple-element.35), channel_id=1, source_target_pairs={{0,1},{1,2},{2,3},{3,4},{4,5},{5,6},{6,7},{7,0},{8,9},{9,10},{10,1... | collective-permute-start | bytes 98312 | tf_op jit(solution)/shard_map/ppermute | solution.py:16
  31.6 11.7 %collective-permute-start.1 = (bf16[16,1024]{1,0:T(8,128)(2,1)S(1)}, bf16[16,1024]{1,0:T(8,128)(2,1)S(1)}, u32[]{:S(2)}, u32[]{:S(2)}) collective-permute-start(bf16[16,1024]{1,0:T(8,128)(2,1)S(1)} %get-tuple-element.34), channel_id=1, source_target_pairs={{0,2},{1,3},{2,4},{3,5},{4,6},{5,7},{6,0},{7,1},{8,10},{9,11},{10,... | collective-permute-start | bytes 98312 | tf_op jit(solution)/shard_map/ppermute | solution.py:16
  34.2 10.5 %collective-permute-start.2 = (bf16[16,1024]{1,0:T(8,128)(2,1)S(1)}, bf16[16,1024]{1,0:T(8,128)(2,1)S(1)}, u32[]{:S(2)}, u32[]{:S(2)}) collective-permute-start(bf16[16,1024]{1,0:T(8,128)(2,1)S(1)} %get-tuple-element.33), channel_id=1, source_target_pairs={{0,3},{1,4},{2,5},{3,6},{4,7},{5,0},{6,1},{7,2},{8,11},{9,12},{10,... | collective-permute-start | bytes 98312 | tf_op jit(solution)/shard_map/ppermute | solution.py:16
  37.4 7.2 %collective-permute-start.3 = (bf16[16,1024]{1,0:T(8,128)(2,1)S(1)}, bf16[16,1024]{1,0:T(8,128)(2,1)S(1)}, u32[]{:S(2)}, u32[]{:S(2)}) collective-permute-start(bf16[16,1024]{1,0:T(8,128)(2,1)S(1)} %get-tuple-element.32), channel_id=1, source_target_pairs={{0,4},{1,5},{2,6},{3,7},{4,0},{5,1},{6,2},{7,3},{8,12},{9,13},{10,... | collective-permute-start | bytes 98312 | tf_op jit(solution)/shard_map/ppermute | solution.py:16
  38.0 6.7 %collective-permute-start.4 = (bf16[16,1024]{1,0:T(8,128)(2,1)S(1)}, bf16[16,1024]{1,0:T(8,128)(2,1)S(1)}, u32[]{:S(2)}, u32[]{:S(2)}) collective-permute-start(bf16[16,1024]{1,0:T(8,128)(2,1)S(1)} %get-tuple-element.31), channel_id=1, source_target_pairs={{0,5},{1,6},{2,7},{3,0},{4,1},{5,2},{6,3},{7,4},{8,13},{9,14},{10,... | collective-permute-start | bytes 98312 | tf_op jit(solution)/shard_map/ppermute | solution.py:16
  40.5 4.4 %collective-permute-start.5 = (bf16[16,1024]{1,0:T(8,128)(2,1)S(1)}, bf16[16,1024]{1,0:T(8,128)(2,1)S(1)}, u32[]{:S(2)}, u32[]{:S(2)}) collective-permute-start(bf16[16,1024]{1,0:T(8,128)(2,1)S(1)} %get-tuple-element.30), channel_id=1, source_target_pairs={{0,6},{1,7},{2,0},{3,1},{4,2},{5,3},{6,4},{7,5},{8,14},{9,15},{10,... | collective-permute-start | bytes 98312 | tf_op jit(solution)/shard_map/ppermute | solution.py:16
  43.3 2.8 %collective-permute-start.6 = (bf16[16,1024]{1,0:T(8,128)(2,1)S(1)}, bf16[16,1024]{1,0:T(8,128)(2,1)S(1)}, u32[]{:S(2)}, u32[]{:S(2)}) collective-permute-start(bf16[16,1024]{1,0:T(8,128)(2,1)S(1)} %get-tuple-element.29), channel_id=1, source_target_pairs={{0,7},{1,0},{2,1},{3,2},{4,3},{5,4},{6,5},{7,6},{8,15},{9,8},{10,9... | collective-permute-start | bytes 98312 | tf_op jit(solution)/shard_map/ppermute | solution.py:16
  49.2 8.9 %copy-start.8 = (s32[1,6]{1,0:T(1,128)S(1)}, s32[1,6]{1,0:T(1,128)}, u32[]{:S(2)}) copy-start(s32[1,6]{1,0:T(1,128)} %param.6) | copy-start | bytes 76
  49.2 9.1 %copy-start.7 = (s32[1,6]{1,0:T(1,128)S(1)}, s32[1,6]{1,0:T(1,128)}, u32[]{:S(2)}) copy-start(s32[1,6]{1,0:T(1,128)} %param.7) | copy-start | bytes 76
  49.2 103.9 %all-to-all-start.1 = ((bf16[32,4,16,1024]{3,2,1,0:T(8,128)(2,1)}), bf16[32,4,16,1024]{3,2,1,0:T(8,128)(2,1)}, u32[]{:S(2)}, u32[]{:S(2)}) async-start(bf16[32,4,16,1024]{3,2,1,0:T(8,128)(2,1)} %bitcast.103), calls=%async_computation.1 | async-start | bytes 8388608 | tf_op jit(solution)/shard_map/all_to_all | solution.py:100
  58.1 14.8 %collective-permute-start.8 = (bf16[1024,256]{1,0:T(8,128)(2,1)S(1)}, bf16[1024,256]{1,0:T(8,128)(2,1)S(1)}, u32[]{:S(2)}, u32[]{:S(2)}) collective-permute-start(bf16[1024,256]{1,0:T(8,128)(2,1)S(1)} %bitcast.114), channel_id=1, source_target_pairs={{0,1},{1,2},{2,3},{3,0},{4,5},{5,6},{6,7},{7,4},{8,9},{9,10},{10,1... | collective-permute-start | bytes 1572872 | tf_op jit(solution)/shard_map/ppermute | solution.py:85
  58.3 26.8 %collective-permute-start.9 = (bf16[1024,256]{1,0:T(8,128)(2,1)S(1)}, bf16[1024,256]{1,0:T(8,128)(2,1)S(1)}, u32[]{:S(2)}, u32[]{:S(2)}) collective-permute-start(bf16[1024,256]{1,0:T(8,128)(2,1)S(1)} %bitcast.115), channel_id=1, source_target_pairs={{0,2},{1,3},{2,0},{3,1},{4,6},{5,7},{6,4},{7,5},{8,10},{9,11},{10,... | collective-permute-start | bytes 1572872 | tf_op jit(solution)/shard_map/ppermute | solution.py:85
  62.5 25.1 %collective-permute-start.10 = (bf16[1024,256]{1,0:T(8,128)(2,1)S(1)}, bf16[1024,256]{1,0:T(8,128)(2,1)S(1)}, u32[]{:S(2)}, u32[]{:S(2)}) collective-permute-start(bf16[1024,256]{1,0:T(8,128)(2,1)S(1)} %bitcast.116), channel_id=1, source_target_pairs={{0,3},{1,0},{2,1},{3,2},{4,7},{5,4},{6,5},{7,6},{8,11},{9,8},{10,9... | collective-permute-start | bytes 1572872 | tf_op jit(solution)/shard_map/ppermute | solution.py:85
  62.6 30.6 %collective-permute-start.11 = (bf16[1024,256]{1,0:T(8,128)(2,1)S(1)}, bf16[1024,256]{1,0:T(8,128)(2,1)S(1)}, u32[]{:S(2)}, u32[]{:S(2)}) collective-permute-start(bf16[1024,256]{1,0:T(8,128)(2,1)S(1)} %bitcast.117), channel_id=1, source_target_pairs={{0,4},{1,5},{2,6},{3,7},{4,0},{5,1},{6,2},{7,3},{8,12},{9,13},{10,... | collective-permute-start | bytes 1572872 | tf_op jit(solution)/shard_map/ppermute | solution.py:87
  72.9 37.1 %collective-permute-start.12 = (bf16[1024,256]{1,0:T(8,128)(2,1)S(1)}, bf16[1024,256]{1,0:T(8,128)(2,1)S(1)}, u32[]{:S(2)}, u32[]{:S(2)}) collective-permute-start(bf16[1024,256]{1,0:T(8,128)(2,1)S(1)} %collective-permute-done.8), channel_id=1, source_target_pairs={{0,4},{1,5},{2,6},{3,7},{4,0},{5,1},{6,2},{7,3},{8,12},{9,13},{10,... | collective-permute-start | bytes 1572872 | tf_op jit(solution)/shard_map/ppermute | solution.py:87
  85.1 51.1 %collective-permute-start.13 = (bf16[1024,256]{1,0:T(8,128)(2,1)S(1)}, bf16[1024,256]{1,0:T(8,128)(2,1)S(1)}, u32[]{:S(2)}, u32[]{:S(2)}) collective-permute-start(bf16[1024,256]{1,0:T(8,128)(2,1)S(1)} %collective-permute-done.9), channel_id=1, source_target_pairs={{0,4},{1,5},{2,6},{3,7},{4,0},{5,1},{6,2},{7,3},{8,12},{9,13},{10,... | collective-permute-start | bytes 1572872 | tf_op jit(solution)/shard_map/ppermute | solution.py:87
  87.6 61.5 %collective-permute-start.14 = (bf16[1024,256]{1,0:T(8,128)(2,1)S(1)}, bf16[1024,256]{1,0:T(8,128)(2,1)S(1)}, u32[]{:S(2)}, u32[]{:S(2)}) collective-permute-start(bf16[1024,256]{1,0:T(8,128)(2,1)S(1)} %collective-permute-done.10), channel_id=1, source_target_pairs={{0,4},{1,5},{2,6},{3,7},{4,0},{5,1},{6,2},{7,3},{8,12},{9,13},{10,... | collective-permute-start | bytes 1572872 | tf_op jit(solution)/shard_map/ppermute | solution.py:87
  158.2 1.7 copy-start.4
  163.5 10.8 %collective-permute-start.7 = (bf16[32,4,16,1024]{3,2,1,0:T(8,128)(2,1)}, bf16[32,4,16,1024]{3,2,1,0:T(8,128)(2,1)}, u32[]{:S(2)}, u32[]{:S(2)}) collective-permute-start(bf16[32,4,16,1024]{3,2,1,0:T(8,128)(2,1)} %all-to-all-done.1), channel_id=1, source_target_pairs={{0,8},{8,0},{1,9},{9,1},{2,10},{10,2},{3,11},{11,3},{4,12},{12,4},... | collective-permute-start | bytes 12582920 | tf_op jit(solution)/shard_map/ppermute | solution.py:101
  179.4 1.8 copy-start.5
  182.3 1.7 copy-start.3
  185.8 2.6 %copy-start.9 = (f32[1632,256]{1,0:T(8,128)S(1)}, f32[1632,256]{1,0:T(8,128)}, u32[]{:S(2)}) copy-start(f32[1632,256]{1,0:T(8,128)} %fusion) | copy-start | bytes 5013508
  (3 other events, 5.0 us)

commit v6 on v5

--- a/solution.py
+++ b/solution.py
@@ -8,12 +8,6 @@
 
 VIRTUAL_SOURCES = 128
 MAXIMUM_LAG = 8
-
-
-def shifted(block, axis, distance):
-    devices = range(lax.axis_size(axis))
-    route = [(i, (i + distance) % len(devices)) for i in devices]
-    return lax.ppermute(block, axis, route)
 
 
 def band_filter(values, taps):
@@ -69,13 +63,8 @@
     sources = lax.dot_general(
         pick, receivers, (((1,), (1,)), ((), ())), preferred_element_type=jnp.float32
     ).astype(receivers.dtype).reshape(n_win, group, samples)
-    source_pieces = [lax.dynamic_index_in_dim(sources, me, 0, keepdims=False)]
+    sources = lax.all_to_all(sources, "win", 0, 0, tiled=True)
     receiver_pieces = [receivers]
-    for distance in range(1, n_win):
-        target = lax.rem(me + distance, n_win)
-        source_pieces.append(
-            shifted(lax.dynamic_index_in_dim(sources, target, 0, keepdims=False), "win", distance)
-        )
 
     ring = n_win // 2
     x_part = me // ring
@@ -88,8 +77,7 @@
     stack = jnp.stack(receiver_pieces + far_pieces)
     position = jnp.arange(n_win, dtype=jnp.int32)
     window_of = ((x_part + position // ring) % 2) * ring + (y_part - position % ring + ring) % ring
-    piece_of = lax.rem(me - window_of + n_win, n_win)
-    panel = jnp.take(jnp.stack(source_pieces), piece_of, axis=0, mode="clip")
+    panel = jnp.take(sources, window_of, axis=0, mode="clip")
 
     core = lax.axis_index("core")
     half = n_win // n_core

time: 247 us -> 241 us (0.976)
  starting transfers between devices: 47.1 us -> 31.9 us
  waiting for transfers between devices: 95.7 us -> 108 us
  blocking collectives: 29.5 us -> 25.9 us
    ppermute x7 -> x0, starting transfers between devices: 14.4 us -> none  [shifted(): return lax.ppermute(block, axis, route)]
    all_to_all x0 -> x1, waiting for transfers between devices: none -> 7.55 us  [on_device(): sources = lax.all_to_all(sources, 'win', 0, 0, tiled=True)]
    all_to_all x0 -> x1, starting transfers between devices: none -> 6.36 us  [on_device(): sources = lax.all_to_all(sources, 'win', 0, 0, tiled=True)]
    ppermute x3, waiting for transfers between devices: 17.1 us -> 21.8 us  [on_device(): receiver_pieces.append(lax.ppermute(receivers, 'win', route))]
    ppermute x4, starting transfers between devices: 8.35 us -> 3.97 us  [on_device(): far_pieces = [lax.ppermute(one, 'win', flip) for one in receiver_pieces]]
    all_to_all x1, blocking collectives: 29.5 us -> 25.9 us  [on_device(): result = lax.all_to_all(result, 'win', 0, 0, tiled=True)]
    unnamed x150 -> x144, local copies, waits for them, and re-layouts: 20.3 us -> 20.3 us
  transfers between devices with their start and end apart: 17 -> 11, of which waited for: 10 -> 8; matrix products, arithmetic and copies ran while one was open for 5% -> 6% of each run, Pallas kernels for 0% -> 0%
where the time goes in v6:
time: 241 us; the launch traced here: 238 us
  waiting for transfers between devices  108 us (45%)
  local copies, waits for them, and re-layouts  54.4 us (23%)
  starting transfers between devices  31.9 us (13%)
  blocking collectives  25.9 us (11%)
  matrix products  16.4 us (7%)
    ppermute x4, waiting for transfers between devices, on_device(): far_pieces = [lax.ppermute(one, 'win', flip) for one in receiver_pieces]  61.6 us
    all_to_all x1, blocking collectives, on_device(): result = lax.all_to_all(result, 'win', 0, 0, tiled=True)  25.9 us
    ppermute x3, waiting for transfers between devices, on_device(): receiver_pieces.append(lax.ppermute(receivers, 'win', route))  21.8 us
    unnamed x144, local copies, waits for them, and re-layouts  20.3 us
    dot_general x2, matrix products, on_device(): lax.dot_general(lagged, lax.dynamic_index_in_dim(stack, which, 0, keepdim...  14.5 us
    all_to_all x1, waiting for transfers between devices, on_device(): gathered = lax.all_to_all(blocks_first, blocks_axis, 0, 0, tiled=True)  14.3 us
    all_to_all x1, starting transfers between devices, on_device(): gathered = lax.all_to_all(blocks_first, blocks_axis, 0, 0, tiled=True)  9.94 us
    all_to_all x1, waiting for transfers between devices, on_device(): sources = lax.all_to_all(sources, 'win', 0, 0, tiled=True)  7.55 us
  transfers between devices with their start and end apart: 11, of which 8 were waited for; matrix products, arithmetic and copies ran while one was open for 6% of the time, Pallas kernels for 0%

profile of v6, /device:TPU:33, one launch (start us, length us, event | category | flops | bytes accessed | tf_op | source)
XLA Modules:
  0.0 237.7 jit_solution(13698922014014486499)
XLA Ops:
  2.3 9.9 %all-to-all-start = ((bf16[32,32,256]{2,1,0:T(8,128)(2,1)}), bf16[32,32,256]{2,1,0:T(8,128)(2,1)S(1)}, u32[]{:S(2)}, u32[]{:S(2)}) async-start(bf16[32,32,256]{2,1,0:T(8,128)(2,1)} %copy.26), calls=%async_computation | async-start | bytes 1048576 | tf_op jit(solution)/shard_map/all_to_all | solution.py:54
  14.4 14.3 %all-to-all-done = bf16[32,32,256]{2,1,0:T(8,128)(2,1)S(1)} async-done(((bf16[32,32,256]{2,1,0:T(8,128)(2,1)}), bf16[32,32,256]{2,1,0:T(8,128)(2,1)S(1)}, u32[]{:S(2)}, u32[]{:S(2)}) %all-to-all-start) | async-done | bytes 524320 | tf_op jit(solution)/shard_map/all_to_all | solution.py:54
  30.8 6.4 %all-to-all-start.1 = ((bf16[8,16,1024]{2,1,0:T(8,128)(2,1)}), bf16[8,16,1024]{2,1,0:T(8,128)(2,1)S(1)}, u32[]{:S(2)}, u32[]{:S(2)}) async-start(bf16[8,16,1024]{2,1,0:T(8,128)(2,1)} %bitcast.12), calls=%async_computation.1 | async-start | bytes 524288 | tf_op jit(solution)/shard_map/all_to_all | solution.py:66
  37.2 7.5 %all-to-all-done.1 = bf16[8,16,1024]{2,1,0:T(8,128)(2,1)S(1)} async-done(((bf16[8,16,1024]{2,1,0:T(8,128)(2,1)}), bf16[8,16,1024]{2,1,0:T(8,128)(2,1)S(1)}, u32[]{:S(2)}, u32[]{:S(2)}) %all-to-all-start.1) | async-done | bytes 262176 | tf_op jit(solution)/shard_map/all_to_all | solution.py:66
  45.4 2.6 %broadcast_in_dim.12 = bf16[16,2,4,16,1024]{4,3,2,1,0:T(8,128)(2,1)} broadcast(bf16[2,4,16,1024]{3,2,1,0:T(8,128)(2,1)S(1)} %bitcast.92), dimensions={1,2,3,4} | broadcast | bytes 4456448 | tf_op jit(solution)/shard_map/broadcast_in_dim | solution.py:85
  47.9 7.5 %all-to-all-start.2 = ((bf16[32,4,16,1024]{3,2,1,0:T(8,128)(2,1)}), bf16[32,4,16,1024]{3,2,1,0:T(8,128)(2,1)}, u32[]{:S(2)}, u32[]{:S(2)}) async-start(bf16[32,4,16,1024]{3,2,1,0:T(8,128)(2,1)} %bitcast.75), calls=%async_computation.2 | async-start | bytes 8388608 | tf_op jit(solution)/shard_map/all_to_all | solution.py:88
  55.6 1.7 collective-permute-start.2
  59.3 21.8 %collective-permute-done.1 = bf16[1024,256]{1,0:T(8,128)(2,1)S(1)} collective-permute-done((bf16[1024,256]{1,0:T(8,128)(2,1)S(1)}, bf16[1024,256]{1,0:T(8,128)(2,1)S(1)}, u32[]{:S(2)}, u32[]{:S(2)}) %collective-permute-start.1) | collective-permute-done | bytes 524320 | tf_op jit(solution)/shard_map/ppermute | solution.py:74
  81.2 3.1 %collective-permute-start.6 = (bf16[1024,256]{1,0:T(8,128)(2,1)S(1)}, bf16[1024,256]{1,0:T(8,128)(2,1)S(1)}, u32[]{:S(2)}, u32[]{:S(2)}) collective-permute-start(bf16[1024,256]{1,0:T(8,128)(2,1)S(1)} %collective-permute-done.2), channel_id=1, source_target_pairs={{0,4},{1,5},{2,6},{3,7},{4,0},{5,1},{6,2},{7,3},{8,12},{9,13},{10,... | collective-permute-start | bytes 1572872 | tf_op jit(solution)/shard_map/ppermute | solution.py:76
  84.6 5.8 %collective-permute-done.4 = bf16[1024,256]{1,0:T(8,128)(2,1)S(1)} collective-permute-done((bf16[1024,256]{1,0:T(8,128)(2,1)S(1)}, bf16[1024,256]{1,0:T(8,128)(2,1)S(1)}, u32[]{:S(2)}, u32[]{:S(2)}) %collective-permute-start.4) | collective-permute-done | bytes 524320 | tf_op jit(solution)/shard_map/ppermute | solution.py:76
  90.5 16.6 %collective-permute-done.5 = bf16[1024,256]{1,0:T(8,128)(2,1)S(1)} collective-permute-done((bf16[1024,256]{1,0:T(8,128)(2,1)S(1)}, bf16[1024,256]{1,0:T(8,128)(2,1)S(1)}, u32[]{:S(2)}, u32[]{:S(2)}) %collective-permute-start.5) | collective-permute-done | bytes 524320 | tf_op jit(solution)/shard_map/ppermute | solution.py:76
  107.1 26.3 %collective-permute-done.6 = bf16[1024,256]{1,0:T(8,128)(2,1)S(1)} collective-permute-done((bf16[1024,256]{1,0:T(8,128)(2,1)S(1)}, bf16[1024,256]{1,0:T(8,128)(2,1)S(1)}, u32[]{:S(2)}, u32[]{:S(2)}) %collective-permute-start.6) | collective-permute-done | bytes 524320 | tf_op jit(solution)/shard_map/ppermute | solution.py:76
  133.4 12.9 %collective-permute-done.7 = bf16[1024,256]{1,0:T(8,128)(2,1)S(1)} collective-permute-done((bf16[1024,256]{1,0:T(8,128)(2,1)S(1)}, bf16[1024,256]{1,0:T(8,128)(2,1)S(1)}, u32[]{:S(2)}, u32[]{:S(2)}) %collective-permute-start.7) | collective-permute-done | bytes 524320 | tf_op jit(solution)/shard_map/ppermute | solution.py:76
  148.0 2.5 %all-to-all-done.2 = bf16[32,4,16,1024]{3,2,1,0:T(8,128)(2,1)} async-done(((bf16[32,4,16,1024]{3,2,1,0:T(8,128)(2,1)}), bf16[32,4,16,1024]{3,2,1,0:T(8,128)(2,1)}, u32[]{:S(2)}, u32[]{:S(2)}) %all-to-all-start.2) | async-done | bytes 4194336 | tf_op jit(solution)/shard_map/all_to_all | solution.py:88
  150.4 2.8 %gather_fusion.1 = bf16[6,4,16,1024]{3,2,1,0:T(8,128)(2,1)S(1)} fusion(bf16[32,4,16,1024]{3,2,1,0:T(8,128)(2,1)} %all-to-all-done.2, s32[1024]{0:T(1024)S(1)} %pad_clamp_fusion), kind=kCustom, calls=%fused_computation.1 | custom fusion | bytes 1572888 | tf_op jit(solution)/shard_map/jit(_take)/gather | solution.py:102
  164.7 7.0 %fusion = f32[1632,256]{1,0:T(8,128)} fusion(bf16[4096,256]{1,0:T(8,128)(2,1)S(1)} %bitcast.83, bf16[1632,1024]{1,0:T(8,128)(2,1)S(1)} %bitcast.98, bf16[1632,1024]{1,0:T(8,128)(2,1)S(1)} %bitcast.97, bf16[1632,1024]{1,0:T(8,128)(2,1)} %bitcast.101, bf16[1632,1024]{1,0:T(8,128)(2,1)} %bitcast.103), kind=kOutput, calls=%fused_computation.3 | convolution fusion | flops 3476029440 | bytes 17137664 | tf_op jit(solution)/shard_map/dot_general | solution.py:109
  171.7 2.8 %gather_fusion.2 = bf16[6,4,16,1024]{3,2,1,0:T(8,128)(2,1)S(1)} fusion(bf16[32,4,16,1024]{3,2,1,0:T(8,128)(2,1)} %collective-permute-done, s32[1024]{0:T(1024)S(1)} %pad_clamp_fusion), kind=kCustom, calls=%fused_computation.2 | custom fusion | bytes 1572888 | tf_op jit(solution)/shard_map/jit(_take)/gather | solution.py:102
  184.1 1.7 copy-done.1
  185.8 7.5 %multiply_bitcast_fusion = f32[256,1632]{0,1:T(8,128)} fusion(f32[1632,256]{1,0:T(8,128)S(1)} %copy-done.9, f32[1632]{0:T(1024)S(1)} %mul.74, bf16[4096,256]{1,0:T(8,128)(2,1)S(1)} %bitcast.82, bf16[1632,1024]{1,0:T(8,128)(2,1)} %bitcast.100, bf16[1632,1024]{1,0:T(8,128)(2,1)S(1)} %bitcast.99, bf16[1632,1024]{1,0:T(8,128)(2,1)} %bitcast.102, ...), kind=kOutput, calls=%fused_computation.19 | convolution fusion | flops 3476865024 | bytes 18815360 | tf_op jit(solution)/shard_map/dot_general | solution.py:109
  193.3 1.8 copy.29
  195.1 25.9 %all_to_all.20 = f32[8,32,1632]{2,1,0:T(8,128)S(1)} all-to-all(f32[8,32,1632]{2,1,0:T(8,128)S(1)} %bitcast.76), channel_id=1, replica_groups=mesh['chips'=16,'core'=2,'win'=8] {'win'}, dimensions={0} | all-to-all | bytes 3342336 | tf_op jit(solution)/shard_map/all_to_all | solution.py:123
  221.0 4.3 %copy.30 = f32[8,32,1632]{1,2,0:T(8,128)} copy(f32[8,32,1632]{2,1,0:T(8,128)S(1)} %all_to_all.20) | data formatting | bytes 3342336 | tf_op jit(solution)/shard_map/all_to_all | solution.py:123
  225.3 6.8 %copy.31 = f32[6,32,17,8,16]{1,4,3,2,0:T(8,128)} copy(f32[6,32,17,8,16]{1,4,2,0,3:T(8,128)} %bitcast.73) | data formatting | bytes 3342336 | tf_op jit(solution)/shard_map/transpose | solution.py:125
  232.0 5.7 %copy.32 = f32[6,32,2176]{2,1,0:T(8,128)} copy(f32[6,32,2176]{1,2,0:T(8,128)} %bitcast.74) | data formatting | bytes 3342336 | tf_op jit(solution)/shard_map/reshape | solution.py:126
  (195 shorter events, 31.5 us)
Async XLA Ops:
  0.0 13.6 %copy-start.6 = (bf16[321]{0:T(512)(128)(2,1)S(1)}, bf16[321]{0:T(512)(128)(2,1)}, u32[]{:S(2)}) copy-start(bf16[321]{0:T(512)(128)(2,1)} %constant.90.clone.1) | copy-start | bytes 1930
  2.3 26.4 %all-to-all-start = ((bf16[32,32,256]{2,1,0:T(8,128)(2,1)}), bf16[32,32,256]{2,1,0:T(8,128)(2,1)S(1)}, u32[]{:S(2)}, u32[]{:S(2)}) async-start(bf16[32,32,256]{2,1,0:T(8,128)(2,1)} %copy.26), calls=%async_computation | async-start | bytes 1048576 | tf_op jit(solution)/shard_map/all_to_all | solution.py:54
  30.8 13.9 %all-to-all-start.1 = ((bf16[8,16,1024]{2,1,0:T(8,128)(2,1)}), bf16[8,16,1024]{2,1,0:T(8,128)(2,1)S(1)}, u32[]{:S(2)}, u32[]{:S(2)}) async-start(bf16[8,16,1024]{2,1,0:T(8,128)(2,1)} %bitcast.12), calls=%async_computation.1 | async-start | bytes 524288 | tf_op jit(solution)/shard_map/all_to_all | solution.py:66
  47.9 7.5 %copy-start.8 = (s32[1,6]{1,0:T(1,128)S(1)}, s32[1,6]{1,0:T(1,128)}, u32[]{:S(2)}) copy-start(s32[1,6]{1,0:T(1,128)} %param.6) | copy-start | bytes 76
  47.9 7.6 %copy-start.7 = (s32[1,6]{1,0:T(1,128)S(1)}, s32[1,6]{1,0:T(1,128)}, u32[]{:S(2)}) copy-start(s32[1,6]{1,0:T(1,128)} %param.7) | copy-start | bytes 76
  47.9 102.5 %all-to-all-start.2 = ((bf16[32,4,16,1024]{3,2,1,0:T(8,128)(2,1)}), bf16[32,4,16,1024]{3,2,1,0:T(8,128)(2,1)}, u32[]{:S(2)}, u32[]{:S(2)}) async-start(bf16[32,4,16,1024]{3,2,1,0:T(8,128)(2,1)} %bitcast.75), calls=%async_computation.2 | async-start | bytes 8388608 | tf_op jit(solution)/shard_map/all_to_all | solution.py:88
  55.4 25.7 %collective-permute-start.1 = (bf16[1024,256]{1,0:T(8,128)(2,1)S(1)}, bf16[1024,256]{1,0:T(8,128)(2,1)S(1)}, u32[]{:S(2)}, u32[]{:S(2)}) collective-permute-start(bf16[1024,256]{1,0:T(8,128)(2,1)S(1)} %bitcast.86), channel_id=1, source_target_pairs={{0,1},{1,2},{2,3},{3,0},{4,5},{5,6},{6,7},{7,4},{8,9},{9,10},{10,1... | collective-permute-start | bytes 1572872 | tf_op jit(solution)/shard_map/ppermute | solution.py:74
  55.6 25.6 %collective-permute-start.2 = (bf16[1024,256]{1,0:T(8,128)(2,1)S(1)}, bf16[1024,256]{1,0:T(8,128)(2,1)S(1)}, u32[]{:S(2)}, u32[]{:S(2)}) collective-permute-start(bf16[1024,256]{1,0:T(8,128)(2,1)S(1)} %bitcast.87), channel_id=1, source_target_pairs={{0,2},{1,3},{2,0},{3,1},{4,6},{5,7},{6,4},{7,5},{8,10},{9,11},{10,... | collective-permute-start | bytes 1572872 | tf_op jit(solution)/shard_map/ppermute | solution.py:74
  57.6 26.7 %collective-permute-start.3 = (bf16[1024,256]{1,0:T(8,128)(2,1)S(1)}, bf16[1024,256]{1,0:T(8,128)(2,1)S(1)}, u32[]{:S(2)}, u32[]{:S(2)}) collective-permute-start(bf16[1024,256]{1,0:T(8,128)(2,1)S(1)} %bitcast.88), channel_id=1, source_target_pairs={{0,3},{1,0},{2,1},{3,2},{4,7},{5,4},{6,5},{7,6},{8,11},{9,8},{10,9... | collective-permute-start | bytes 1572872 | tf_op jit(solution)/shard_map/ppermute | solution.py:74
  58.7 31.8 %collective-permute-start.4 = (bf16[1024,256]{1,0:T(8,128)(2,1)S(1)}, bf16[1024,256]{1,0:T(8,128)(2,1)S(1)}, u32[]{:S(2)}, u32[]{:S(2)}) collective-permute-start(bf16[1024,256]{1,0:T(8,128)(2,1)S(1)} %bitcast.89), channel_id=1, source_target_pairs={{0,4},{1,5},{2,6},{3,7},{4,0},{5,1},{6,2},{7,3},{8,12},{9,13},{10,... | collective-permute-start | bytes 1572872 | tf_op jit(solution)/shard_map/ppermute | solution.py:76
  81.1 26.0 %collective-permute-start.5 = (bf16[1024,256]{1,0:T(8,128)(2,1)S(1)}, bf16[1024,256]{1,0:T(8,128)(2,1)S(1)}, u32[]{:S(2)}, u32[]{:S(2)}) collective-permute-start(bf16[1024,256]{1,0:T(8,128)(2,1)S(1)} %collective-permute-done.1), channel_id=1, source_target_pairs={{0,4},{1,5},{2,6},{3,7},{4,0},{5,1},{6,2},{7,3},{8,12},{9,13},{10,... | collective-permute-start | bytes 1572872 | tf_op jit(solution)/shard_map/ppermute | solution.py:76
  81.2 52.2 %collective-permute-start.6 = (bf16[1024,256]{1,0:T(8,128)(2,1)S(1)}, bf16[1024,256]{1,0:T(8,128)(2,1)S(1)}, u32[]{:S(2)}, u32[]{:S(2)}) collective-permute-start(bf16[1024,256]{1,0:T(8,128)(2,1)S(1)} %collective-permute-done.2), channel_id=1, source_target_pairs={{0,4},{1,5},{2,6},{3,7},{4,0},{5,1},{6,2},{7,3},{8,12},{9,13},{10,... | collective-permute-start | bytes 1572872 | tf_op jit(solution)/shard_map/ppermute | solution.py:76
  84.3 62.0 %collective-permute-start.7 = (bf16[1024,256]{1,0:T(8,128)(2,1)S(1)}, bf16[1024,256]{1,0:T(8,128)(2,1)S(1)}, u32[]{:S(2)}, u32[]{:S(2)}) collective-permute-start(bf16[1024,256]{1,0:T(8,128)(2,1)S(1)} %collective-permute-done.3), channel_id=1, source_target_pairs={{0,4},{1,5},{2,6},{3,7},{4,0},{5,1},{6,2},{7,3},{8,12},{9,13},{10,... | collective-permute-start | bytes 1572872 | tf_op jit(solution)/shard_map/ppermute | solution.py:76
  155.5 1.7 copy-start.4
  158.4 1.7 copy-start.2
  160.9 10.8 %collective-permute-start = (bf16[32,4,16,1024]{3,2,1,0:T(8,128)(2,1)}, bf16[32,4,16,1024]{3,2,1,0:T(8,128)(2,1)}, u32[]{:S(2)}, u32[]{:S(2)}) collective-permute-start(bf16[32,4,16,1024]{3,2,1,0:T(8,128)(2,1)} %all-to-all-done.2), channel_id=1, source_target_pairs={{0,8},{8,0},{1,9},{9,1},{2,10},{10,2},{3,11},{11,3},{4,12},{12,4},... | collective-permute-start | bytes 12582920 | tf_op jit(solution)/shard_map/ppermute | solution.py:89
  163.1 1.6 copy-start
  176.7 1.8 copy-start.5
  179.7 1.7 copy-start.3
  183.1 2.6 %copy-start.9 = (f32[1632,256]{1,0:T(8,128)S(1)}, f32[1632,256]{1,0:T(8,128)}, u32[]{:S(2)}) copy-start(f32[1632,256]{1,0:T(8,128)} %fusion) | copy-start | bytes 5013508
  184.1 1.7 copy-start.1
